TPU v7x, 32 devices: a whole 2x2x4 slice. The times are simulated.
32 devices in a mesh: shots: 2 (over x), src: 16 (over z, y, core).
Axes of the slice: x: 2, y: 2, z: 4, core: 2. Of those that a mesh axis runs over, the one named last changes fastest.
Arguments:
- weights_in: float32 [1024, 128, 256], P(('shots', 'src')), parts along dimension 0, may hold values from -6 to 6
- translations: float32 [8, 8, 2, 2, 64, 64], replicated, may hold values from -0.375 to 0.375
- pattern_index: int32 [8, 512], replicated, may hold values from 0 to 7
Outputs:
- weights_out: float32 [1024, 128, 256], P(('shots', 'src')), parts along dimension 0
There are 2 independent parts, one for each index of `shots`. A program takes and returns all parts, laid end to end along the dimension named above; an argument that names none is the same for every part. Nothing has to cross between parts.
All inputs are finite; a program needn't handle non-finite values.
Results may differ from a plain program's by a relative error of at most 0.0001.
Values sent between devices are 32-bit elements; how exact they have to be, the bound alone decides.
No kernel may reach another device: no remote copies, remote signals or barrier semaphores. Data moves between devices by JAX's collectives and lax.ppermute only.
A program may use at most 128 MiB of HBM per device.

v0:
```python
import jax
import jax.numpy as jnp
from jax import lax
from jax.sharding import PartitionSpec as P

LEVELS = 8


def pair_flip(field, bit):
    count = field.shape[0]
    shaped = field.reshape((count // (2 << bit), 2, 1 << bit) + field.shape[1:])
    return jnp.flip(shaped, 1).reshape(field.shape)


def block_real(chosen):
    real_part = chosen[:, :, 0]
    imag_part = chosen[:, :, 1]
    upper = jnp.concatenate([real_part, -imag_part], axis=-1)
    lower = jnp.concatenate([imag_part, real_part], axis=-1)
    return jnp.concatenate([upper, lower], axis=-2)


def apply_level(state, other, table, patterns):
    mats = block_real(jnp.take(table, patterns, axis=0))
    own_term = jnp.einsum("bij,bjk->bik", mats[:, 0], state, precision=lax.Precision.HIGHEST)
    return own_term + jnp.einsum("bij,bjk->bik", mats[:, 1], other, precision=lax.Precision.HIGHEST)


def body(weights_in, translations, pattern_index):
    box_count = weights_in.shape[0]
    groups = lax.axis_size("src")
    local_bits = box_count.bit_length() - 1
    top_bits = (box_count * groups).bit_length() - 1
    device = lax.axis_index("src")
    own_boxes = device * box_count + jnp.arange(box_count, dtype=jnp.int32)
    state = weights_in
    first_cross = LEVELS
    for level in range(LEVELS):
        bit = top_bits - LEVELS + level
        if bit >= local_bits:
            first_cross = level
            break
        patterns = jnp.take(pattern_index[level], own_boxes)
        state = apply_level(state, pair_flip(state, bit), translations[level], patterns)
    repeat = box_count // groups
    repeat_bits = repeat.bit_length() - 1
    slot = jnp.arange(box_count, dtype=jnp.int32)
    held_boxes = slot // repeat * box_count + device * repeat + slot % repeat
    current = lax.all_to_all(state, "src", split_axis=0, concat_axis=0, tiled=True)
    for level in range(first_cross, LEVELS):
        bit = top_bits - LEVELS + level
        patterns = jnp.take(pattern_index[level], held_boxes)
        current = apply_level(
            current,
            pair_flip(current, bit - local_bits + repeat_bits),
            translations[level],
            patterns,
        )
    return lax.all_to_all(current, "src", split_axis=0, concat_axis=0, tiled=True)


def solution(mesh):
    placed = (P(("shots", "src"), None, None), P(), P())
    return jax.shard_map(
        body, mesh=mesh, in_specs=placed, out_specs=P(("shots", "src"), None, None), check_vma=False
    )
```

profile of v0, /device:TPU:15, one launch (start us, length us, event | category | flops | bytes accessed | tf_op | source)
XLA Modules:
  0.0 408.3 jit_solution(616087379427980147)
XLA Ops:
  2.5 6.1 %slice_bitcast_fusion.55 = (f32[8,2,2,64,64]{4,3,2,1,0:T(8,128)S(1)}, f32[8,2,2,64,64]{4,3,2,1,0:T(8,128)}, f32[8,2,2,64,64]{4,3,2,1,0:T(8,128)}, f32[8,2,2,64,6...) fusion(f32[8,8,2,2,64,64]{5,4,3,2,1,0:T(8,128)} %param.8), kind=kLoop, calls=%fused_computation.87 | loop fusion | bytes 8388608 | tf_op jit(solution)/shard_map/squeeze | solution.py:56
  56.1 5.3 %fusion = f32[32,128,256]{2,1,0:T(8,128)} fusion(f32[32,128,256]{2,1,0:T(8,128)S(1)} %copy-done.15, f32[32,2,128,128]{3,2,0,1:T(8,128)S(1)} %maximum_maximum_fusion.7), kind=kOutput, calls=%fused_computation.49 | convolution fusion | flops 1610612736 | bytes 10485760 | tf_op jit(solution)/shard_map/bij,bjk->bik/dot_general | solution.py:25
  66.0 8.7 %convolution_add_fusion.7 = f32[32,128,256]{2,1,0:T(8,128)S(1)} fusion(f32[32,128,256]{2,1,0:T(8,128)} %fusion, f32[32,128,256]{2,1,0:T(8,128)} %bitcast.173, f32[32,2,128,128]{3,2,0,1:T(8,128)} %copy-done.13), kind=kOutput, calls=%fused_computation.39 | convolution fusion | flops 1611661312 | bytes 14680064 | tf_op jit(solution)/shard_map/bij,bjk->bik/dot_general | solution.py:26
  76.6 5.3 %fusion.1 = f32[32,128,256]{2,1,0:T(8,128)} fusion(f32[32,128,256]{2,1,0:T(8,128)S(1)} %convolution_add_fusion.7, f32[32,2,128,128]{3,2,0,1:T(8,128)S(1)} %maximum_maximum_fusion.6), kind=kOutput, calls=%fused_computation.53 | convolution fusion | flops 1610612736 | bytes 10485760 | tf_op jit(solution)/shard_map/bij,bjk->bik/dot_general | solution.py:25
  81.9 4.7 %rev.29 = f32[4,2,4,128,256]{4,3,2,1,0:T(8,128)} reverse(f32[4,2,4,128,256]{4,3,2,1,0:T(8,128)} %bitcast.160), dimensions={1} | reverse | bytes 8388608 | tf_op jit(solution)/shard_map/jit(_flip)/rev | solution.py:12
  86.6 8.7 %convolution_add_fusion.6 = f32[32,128,256]{2,1,0:T(8,128)S(1)} fusion(f32[32,128,256]{2,1,0:T(8,128)} %fusion.1, f32[32,128,256]{2,1,0:T(8,128)} %bitcast.166, f32[32,2,128,128]{3,2,0,1:T(8,128)} %copy-done.10), kind=kOutput, calls=%fused_computation.38 | convolution fusion | flops 1611661312 | bytes 14680064 | tf_op jit(solution)/shard_map/bij,bjk->bik/dot_general | solution.py:26
  97.3 5.5 %fusion.2 = f32[32,128,256]{2,1,0:T(8,128)} fusion(f32[32,128,256]{2,1,0:T(8,128)S(1)} %convolution_add_fusion.6, f32[32,2,128,128]{3,2,0,1:T(8,128)S(1)} %maximum_maximum_fusion.5), kind=kOutput, calls=%fused_computation.57 | convolution fusion | flops 1610612736 | bytes 10485760 | tf_op jit(solution)/shard_map/bij,bjk->bik/dot_general | solution.py:25
  102.8 4.7 %rev.30 = f32[2,2,8,128,256]{4,3,2,1,0:T(8,128)} reverse(f32[2,2,8,128,256]{4,3,2,1,0:T(8,128)} %bitcast.161), dimensions={1} | reverse | bytes 8388608 | tf_op jit(solution)/shard_map/jit(_flip)/rev | solution.py:12
  107.4 8.7 %convolution_add_fusion.5 = f32[32,128,256]{2,1,0:T(8,128)S(1)} fusion(f32[32,128,256]{2,1,0:T(8,128)} %fusion.2, f32[32,128,256]{2,1,0:T(8,128)} %bitcast.167, f32[32,2,128,128]{3,2,0,1:T(8,128)} %copy-done.11), kind=kOutput, calls=%fused_computation.37 | convolution fusion | flops 1611661312 | bytes 14680064 | tf_op jit(solution)/shard_map/bij,bjk->bik/dot_general | solution.py:26
  118.1 5.1 %fusion.3 = f32[32,128,256]{2,1,0:T(8,128)} fusion(f32[32,128,256]{2,1,0:T(8,128)S(1)} %convolution_add_fusion.5, f32[32,2,128,128]{3,2,0,1:T(8,128)S(1)} %maximum_maximum_fusion.4), kind=kOutput, calls=%fused_computation.61 | convolution fusion | flops 1610612736 | bytes 10485760 | tf_op jit(solution)/shard_map/bij,bjk->bik/dot_general | solution.py:25
  123.2 4.7 %rev.31 = f32[1,2,16,128,256]{4,3,2,1,0:T(8,128)} reverse(f32[1,2,16,128,256]{4,3,2,1,0:T(8,128)} %bitcast.162), dimensions={1} | reverse | bytes 8388608 | tf_op jit(solution)/shard_map/jit(_flip)/rev | solution.py:12
  127.9 9.9 %convolution_add_fusion.4 = f32[32,128,256]{2,1,0:T(8,128)} fusion(f32[32,128,256]{2,1,0:T(8,128)} %fusion.3, f32[32,128,256]{2,1,0:T(8,128)} %bitcast.168, f32[32,2,128,128]{3,2,0,1:T(8,128)} %copy-done.12), kind=kOutput, calls=%fused_computation.36 | convolution fusion | flops 1611661312 | bytes 14680064 | tf_op jit(solution)/shard_map/bij,bjk->bik/dot_general | solution.py:26
  137.8 6.6 %all-to-all-start = ((f32[32,128,256]{2,1,0:T(8,128)}), f32[32,128,256]{2,1,0:T(8,128)}, u32[]{:S(2)}, u32[]{:S(2)}) async-start(f32[32,128,256]{2,1,0:T(8,128)} %convolution_add_fusion.4), calls=%async_computation | async-start | bytes 8388608 | tf_op jit(solution)/shard_map/all_to_all | solution.py:49
  179.8 57.0 %all-to-all-done = f32[32,128,256]{2,1,0:T(8,128)} async-done(((f32[32,128,256]{2,1,0:T(8,128)}), f32[32,128,256]{2,1,0:T(8,128)}, u32[]{:S(2)}, u32[]{:S(2)}) %all-to-all-start) | async-done | bytes 4194336 | tf_op jit(solution)/shard_map/all_to_all | solution.py:49
  241.5 7.5 %fusion.4 = f32[32,128,256]{2,1,0:T(8,128)S(1)} fusion(f32[32,128,256]{2,1,0:T(8,128)} %all-to-all-done, f32[32,2,128,128]{3,2,0,1:T(8,128)} %maximum_maximum_fusion.3), kind=kOutput, calls=%fused_computation.65 | convolution fusion | flops 1610612736 | bytes 10485760 | tf_op jit(solution)/shard_map/bij,bjk->bik/dot_general | solution.py:25
  253.4 5.5 %fusion.5 = f32[32,128,256]{2,1,0:T(8,128)} fusion(f32[32,128,256]{2,1,0:T(8,128)S(1)} %convolution_add_fusion.3, f32[32,2,128,128]{3,2,0,1:T(8,128)S(1)} %copy-done.7), kind=kOutput, calls=%fused_computation.69 | convolution fusion | flops 1610612736 | bytes 10485760 | tf_op jit(solution)/shard_map/bij,bjk->bik/dot_general | solution.py:25
  258.9 4.7 %rev.33 = f32[4,2,4,128,256]{4,3,2,1,0:T(8,128)} reverse(f32[4,2,4,128,256]{4,3,2,1,0:T(8,128)} %bitcast.163), dimensions={1} | reverse | bytes 8388608 | tf_op jit(solution)/shard_map/jit(_flip)/rev | solution.py:12
  263.6 8.6 %convolution_add_fusion.2 = f32[32,128,256]{2,1,0:T(8,128)S(1)} fusion(f32[32,128,256]{2,1,0:T(8,128)} %fusion.5, f32[32,128,256]{2,1,0:T(8,128)} %bitcast.170, f32[32,2,128,128]{3,2,0,1:T(8,128)} %maximum_maximum_fusion.2), kind=kOutput, calls=%fused_computation.34 | convolution fusion | flops 1611661312 | bytes 14680064 | tf_op jit(solution)/shard_map/bij,bjk->bik/dot_general | solution.py:26
  272.2 5.1 %fusion.6 = f32[32,128,256]{2,1,0:T(8,128)} fusion(f32[32,128,256]{2,1,0:T(8,128)S(1)} %convolution_add_fusion.2, f32[32,2,128,128]{3,2,0,1:T(8,128)S(1)} %copy-done.8), kind=kOutput, calls=%fused_computation.73 | convolution fusion | flops 1610612736 | bytes 10485760 | tf_op jit(solution)/shard_map/bij,bjk->bik/dot_general | solution.py:25
  277.4 4.7 %rev.34 = f32[2,2,8,128,256]{4,3,2,1,0:T(8,128)} reverse(f32[2,2,8,128,256]{4,3,2,1,0:T(8,128)} %bitcast.164), dimensions={1} | reverse | bytes 8388608 | tf_op jit(solution)/shard_map/jit(_flip)/rev | solution.py:12
  282.0 8.6 %convolution_add_fusion.1 = f32[32,128,256]{2,1,0:T(8,128)S(1)} fusion(f32[32,128,256]{2,1,0:T(8,128)} %fusion.6, f32[32,128,256]{2,1,0:T(8,128)} %bitcast.171, f32[32,2,128,128]{3,2,0,1:T(8,128)} %maximum_maximum_fusion.1), kind=kOutput, calls=%fused_computation.33 | convolution fusion | flops 1611661312 | bytes 14680064 | tf_op jit(solution)/shard_map/bij,bjk->bik/dot_general | solution.py:26
  290.7 5.3 %fusion.7 = f32[32,128,256]{2,1,0:T(8,128)} fusion(f32[32,128,256]{2,1,0:T(8,128)S(1)} %convolution_add_fusion.1, f32[32,2,128,128]{3,2,0,1:T(8,128)S(1)} %copy-done.9), kind=kOutput, calls=%fused_computation.77 | convolution fusion | flops 1610612736 | bytes 10485760 | tf_op jit(solution)/shard_map/bij,bjk->bik/dot_general | solution.py:25
  300.7 8.5 %convolution_add_fusion = f32[32,128,256]{2,1,0:T(8,128)S(1)} fusion(f32[32,128,256]{2,1,0:T(8,128)} %fusion.7, f32[32,128,256]{2,1,0:T(8,128)} %bitcast.172, f32[32,2,128,128]{3,2,0,1:T(8,128)} %maximum_maximum_fusion), kind=kOutput, calls=%fused_computation.32 | convolution fusion | flops 1611661312 | bytes 14680064 | tf_op jit(solution)/shard_map/bij,bjk->bik/dot_general | solution.py:26
  309.2 97.0 %all_to_all.10 = f32[32,128,256]{2,1,0:T(8,128)S(1)} all-to-all(f32[32,128,256]{2,1,0:T(8,128)S(1)} %convolution_add_fusion), channel_id=1, replica_groups=mesh['shots'=2,'src'=16] {'src'}, dimensions={0} | all-to-all | bytes 8388608 | tf_op jit(solution)/shard_map/all_to_all | solution.py:59
  (132 shorter events, 111.3 us)
Async XLA Ops:
  48.7 3.8 copy-start.26
  56.1 5.3 %copy-start.13 = (f32[32,2,128,128]{3,2,0,1:T(8,128)}, f32[32,2,128,128]{3,2,0,1:T(8,128)S(1)}, u32[]{:S(2)}) copy-start(f32[32,2,128,128]{3,2,0,1:T(8,128)S(1)} %maximum_maximum_fusion.7) | copy-start | bytes 12582916
  66.0 8.7 %copy-start.19 = (f32[32,2,64,64]{3,2,0,1:T(8,128)S(1)}, f32[32,2,64,64]{3,2,0,1:T(8,128)}, u32[]{:S(2)}) copy-start(f32[32,2,64,64]{3,2,0,1:T(8,128)} %fusion.17) | copy-start | bytes 3145732
  66.0 8.7 %copy-start.23 = (f32[32,2,64,64]{3,2,0,1:T(8,128)S(1)}, f32[32,2,64,64]{3,2,0,1:T(8,128)}, u32[]{:S(2)}) copy-start(f32[32,2,64,64]{3,2,0,1:T(8,128)} %get-tuple-element.43) | copy-start | bytes 3145732
  66.0 8.7 %copy-start.24 = (f32[32,2,64,64]{3,2,0,1:T(8,128)S(1)}, f32[32,2,64,64]{3,2,0,1:T(8,128)}, u32[]{:S(2)}) copy-start(f32[32,2,64,64]{3,2,0,1:T(8,128)} %get-tuple-element.44) | copy-start | bytes 3145732
  76.6 5.3 %copy-start.10 = (f32[32,2,128,128]{3,2,0,1:T(8,128)}, f32[32,2,128,128]{3,2,0,1:T(8,128)S(1)}, u32[]{:S(2)}) copy-start(f32[32,2,128,128]{3,2,0,1:T(8,128)S(1)} %maximum_maximum_fusion.6) | copy-start | bytes 12582916
  86.6 8.7 %copy-start.21 = (f32[32,2,64,64]{3,2,0,1:T(8,128)S(1)}, f32[32,2,64,64]{3,2,0,1:T(8,128)}, u32[]{:S(2)}) copy-start(f32[32,2,64,64]{3,2,0,1:T(8,128)} %fusion.16) | copy-start | bytes 3145732
  86.6 8.7 %copy-start.27 = (f32[32,2,64,64]{3,2,0,1:T(8,128)S(1)}, f32[32,2,64,64]{3,2,0,1:T(8,128)}, u32[]{:S(2)}) copy-start(f32[32,2,64,64]{3,2,0,1:T(8,128)} %get-tuple-element.41) | copy-start | bytes 3145732
  86.6 8.7 %copy-start.28 = (f32[32,2,64,64]{3,2,0,1:T(8,128)S(1)}, f32[32,2,64,64]{3,2,0,1:T(8,128)}, u32[]{:S(2)}) copy-start(f32[32,2,64,64]{3,2,0,1:T(8,128)} %get-tuple-element.42) | copy-start | bytes 3145732
  97.3 5.5 %copy-start.11 = (f32[32,2,128,128]{3,2,0,1:T(8,128)}, f32[32,2,128,128]{3,2,0,1:T(8,128)S(1)}, u32[]{:S(2)}) copy-start(f32[32,2,128,128]{3,2,0,1:T(8,128)S(1)} %maximum_maximum_fusion.5) | copy-start | bytes 12582916
  107.4 8.7 %copy-start.22 = (f32[32,2,64,64]{3,2,0,1:T(8,128)S(1)}, f32[32,2,64,64]{3,2,0,1:T(8,128)}, u32[]{:S(2)}) copy-start(f32[32,2,64,64]{3,2,0,1:T(8,128)} %fusion.15) | copy-start | bytes 3145732
  107.4 8.7 %copy-start.29 = (f32[32,2,64,64]{3,2,0,1:T(8,128)S(1)}, f32[32,2,64,64]{3,2,0,1:T(8,128)}, u32[]{:S(2)}) copy-start(f32[32,2,64,64]{3,2,0,1:T(8,128)} %get-tuple-element.39) | copy-start | bytes 3145732
  107.4 8.7 %copy-start.30 = (f32[32,2,64,64]{3,2,0,1:T(8,128)S(1)}, f32[32,2,64,64]{3,2,0,1:T(8,128)}, u32[]{:S(2)}) copy-start(f32[32,2,64,64]{3,2,0,1:T(8,128)} %get-tuple-element.40) | copy-start | bytes 3145732
  118.1 5.1 %copy-start.12 = (f32[32,2,128,128]{3,2,0,1:T(8,128)}, f32[32,2,128,128]{3,2,0,1:T(8,128)S(1)}, u32[]{:S(2)}) copy-start(f32[32,2,128,128]{3,2,0,1:T(8,128)S(1)} %maximum_maximum_fusion.4) | copy-start | bytes 12582916
  137.8 99.0 %all-to-all-start = ((f32[32,128,256]{2,1,0:T(8,128)}), f32[32,128,256]{2,1,0:T(8,128)}, u32[]{:S(2)}, u32[]{:S(2)}) async-start(f32[32,128,256]{2,1,0:T(8,128)} %convolution_add_fusion.4), calls=%async_computation | async-start | bytes 8388608 | tf_op jit(solution)/shard_map/all_to_all | solution.py:49
  172.1 3.2 copy-start.16
  241.4 7.5 %copy-start.6 = (f32[32,2,128,128]{3,2,0,1:T(8,128)S(1)}, f32[32,2,128,128]{3,2,0,1:T(8,128)}, u32[]{:S(2)}) copy-start(f32[32,2,128,128]{3,2,0,1:T(8,128)} %maximum_maximum_fusion.3) | copy-start | bytes 12582916
  241.4 7.5 %copy-start.14 = (f32[8,2,2,128,256]{4,3,2,1,0:T(8,128)S(1)}, f32[8,2,2,128,256]{4,3,2,1,0:T(8,128)}, u32[]{:S(2)}) copy-start(f32[8,2,2,128,256]{4,3,2,1,0:T(8,128)} %rev.32) | copy-start | bytes 12582916
  249.0 4.4 %copy-start.7 = (f32[32,2,128,128]{3,2,0,1:T(8,128)S(1)}, f32[32,2,128,128]{3,2,0,1:T(8,128)}, u32[]{:S(2)}) copy-start(f32[32,2,128,128]{3,2,0,1:T(8,128)} %maximum_maximum_fusion.2) | copy-start | bytes 12582916
  253.4 5.5 %copy-start.3 = (f32[32,128,256]{2,1,0:T(8,128)}, f32[32,128,256]{2,1,0:T(8,128)S(1)}, u32[]{:S(2)}) copy-start(f32[32,128,256]{2,1,0:T(8,128)S(1)} %convolution_add_fusion.3) | copy-start | bytes 12582916
  263.6 8.6 %copy-start.8 = (f32[32,2,128,128]{3,2,0,1:T(8,128)S(1)}, f32[32,2,128,128]{3,2,0,1:T(8,128)}, u32[]{:S(2)}) copy-start(f32[32,2,128,128]{3,2,0,1:T(8,128)} %maximum_maximum_fusion.1) | copy-start | bytes 12582916
  272.2 5.1 %copy-start.4 = (f32[32,128,256]{2,1,0:T(8,128)}, f32[32,128,256]{2,1,0:T(8,128)S(1)}, u32[]{:S(2)}) copy-start(f32[32,128,256]{2,1,0:T(8,128)S(1)} %convolution_add_fusion.2) | copy-start | bytes 12582916
  282.0 8.6 %copy-start.9 = (f32[32,2,128,128]{3,2,0,1:T(8,128)S(1)}, f32[32,2,128,128]{3,2,0,1:T(8,128)}, u32[]{:S(2)}) copy-start(f32[32,2,128,128]{3,2,0,1:T(8,128)} %maximum_maximum_fusion) | copy-start | bytes 12582916
  290.7 5.3 %copy-start.5 = (f32[32,128,256]{2,1,0:T(8,128)}, f32[32,128,256]{2,1,0:T(8,128)S(1)}, u32[]{:S(2)}) copy-start(f32[32,128,256]{2,1,0:T(8,128)S(1)} %convolution_add_fusion.1) | copy-start | bytes 12582916
  (8 other events, 19.6 us)
where the time goes:
time: 416 us; the launch traced here: 408 us
  matrix products  111 us (27%)
  blocking collectives  97 us (23%)
  local copies, waits for them, and re-layouts  96.8 us (23%)
  waiting for transfers between devices  57 us (14%)
  other arithmetic  39.5 us (9%)
  starting transfers between devices  6.56 us (2%)
    all_to_all x1, blocking collectives, body(): lax.all_to_all(current, 'src', split_axis=0, concat_axis=0, tiled=True)  97 us
    dot_general x8, matrix products, apply_level(): jnp.einsum('bij,bjk->bik', mats[:, 1], other, precision=lax.Precision.HIG...  66.1 us
    all_to_all x1, waiting for transfers between devices, body(): lax.all_to_all(state, 'src', split_axis=0, concat_axis=0, tiled=True)  57 us
    dot_general x8, matrix products, apply_level(): jnp.einsum('bij,bjk->bik', mats[:, 0], state, precision=lax.Precision.HIG...  44.6 us
    rev x8, local copies, waits for them, and re-layouts, pair_flip(): return jnp.flip(shaped, 1).reshape(field.shape)  37.2 us
    gather x8, local copies, waits for them, and re-layouts, apply_level(): mats = block_real(jnp.take(table, patterns, axis=0))  28.6 us
    concatenate x8, other arithmetic, block_real(): return jnp.concatenate([upper, lower], axis=-2)  17.1 us
    select_n x8, other arithmetic, apply_level(): mats = block_real(jnp.take(table, patterns, axis=0))  15.3 us
  transfers between devices with their start and end apart: 1, of which 1 were waited for; matrix products, arithmetic and copies ran while one was open for 9% of the time, Pallas kernels for 0%

commit v1 on v0

v1 whole, which is shorter than its diff:
```python
import functools

import jax
import jax.numpy as jnp
from jax import lax
from jax.experimental import pallas as pl
from jax.experimental.pallas import tpu as pltpu
from jax.sharding import PartitionSpec as P

LEVELS = 8
K_CHUNKS = 2


def block_real_table(translations):
    real_part = translations[:, :, :, 0]
    imag_part = translations[:, :, :, 1]
    upper = jnp.concatenate([real_part, -imag_part], axis=-1)
    lower = jnp.concatenate([imag_part, real_part], axis=-1)
    return jnp.concatenate([upper, lower], axis=-2)


def levels_kernel(masks, pidx_ref, m_ref, x_ref, o_ref, buf):
    count = x_ref.shape[0]
    src = x_ref
    for li, mask in enumerate(masks):
        dst = o_ref if li == len(masks) - 1 else buf.at[li % 2]

        def pair(i, carry, src=src, dst=dst, li=li, mask=mask):
            lo = (i // mask) * (2 * mask) + i % mask
            hi = lo + mask
            p_lo = pidx_ref[li, lo]
            p_hi = pidx_ref[li, hi]
            lhs = jnp.concatenate(
                [
                    jnp.concatenate([m_ref[li, p_lo, 0], m_ref[li, p_lo, 1]], axis=1),
                    jnp.concatenate([m_ref[li, p_hi, 1], m_ref[li, p_hi, 0]], axis=1),
                ],
                axis=0,
            )
            rhs = jnp.concatenate([src[lo], src[hi]], axis=0)
            out = jnp.dot(lhs, rhs, precision=lax.Precision.HIGHEST, preferred_element_type=jnp.float32)
            half = out.shape[0] // 2
            dst[lo] = out[:half]
            dst[hi] = out[half:]
            return carry

        lax.fori_loop(0, count // 2, pair, 0)
        src = dst


def apply_levels(state, mats, pidx, masks, chunk, width):
    count, rows, _ = state.shape
    n_levels = mats.shape[0]
    kernel = functools.partial(levels_kernel, tuple(masks))
    flops = 2 * count * rows * 2 * rows * width * n_levels
    return pl.pallas_call(
        kernel,
        out_shape=jax.ShapeDtypeStruct((count, rows, width), state.dtype),
        grid_spec=pltpu.PrefetchScalarGridSpec(
            num_scalar_prefetch=1,
            grid=(1,),
            in_specs=[
                pl.BlockSpec(mats.shape, lambda i, p: (0,) * mats.ndim),
                pl.BlockSpec((count, rows, width), lambda i, p: (0, 0, chunk)),
            ],
            out_specs=pl.BlockSpec((count, rows, width), lambda i, p: (0, 0, 0)),
            scratch_shapes=[pltpu.VMEM((2, count, rows, width), jnp.float32)],
        ),
        compiler_params=pltpu.CompilerParams(vmem_limit_bytes=60 * 1024 * 1024),
        cost_estimate=pl.CostEstimate(
            flops=flops, transcendentals=0, bytes_accessed=2 * count * rows * width * 4 + mats.size * 4
        ),
    )(pidx, mats, state)


def body(weights_in, translations, pattern_index):
    box_count, rows, k_len = weights_in.shape
    groups = lax.axis_size("src")
    local_bits = box_count.bit_length() - 1
    top_bits = (box_count * groups).bit_length() - 1
    device = lax.axis_index("src")
    mats = block_real_table(translations)
    bits = [top_bits - LEVELS + level for level in range(LEVELS)]
    first_cross = next((lv for lv, b in enumerate(bits) if b >= local_bits), LEVELS)

    own_boxes = device * box_count + jnp.arange(box_count, dtype=jnp.int32)
    repeat = box_count // groups
    repeat_bits = repeat.bit_length() - 1
    slot = jnp.arange(box_count, dtype=jnp.int32)
    held_boxes = slot // repeat * box_count + device * repeat + slot % repeat

    width = k_len // K_CHUNKS
    local_masks = [1 << bits[lv] for lv in range(first_cross)]
    cross_masks = [1 << (bits[lv] - local_bits + repeat_bits) for lv in range(first_cross, LEVELS)]
    local_pidx = jnp.take(pattern_index[:first_cross], own_boxes, axis=1)
    cross_pidx = jnp.take(pattern_index[first_cross:], held_boxes, axis=1)

    pieces = []
    for chunk in range(K_CHUNKS):
        if first_cross > 0:
            state = apply_levels(weights_in, mats[:first_cross], local_pidx, local_masks, chunk, width)
            src_chunk = 0
        else:
            state = weights_in
            src_chunk = chunk
        current = lax.all_to_all(state, "src", split_axis=0, concat_axis=0, tiled=True)
        current = apply_levels(current, mats[first_cross:], cross_pidx, cross_masks, src_chunk, width)
        pieces.append(lax.all_to_all(current, "src", split_axis=0, concat_axis=0, tiled=True))
    return jnp.concatenate(pieces, axis=-1)


def solution(mesh):
    placed = (P(("shots", "src"), None, None), P(), P())
    return jax.shard_map(
        body, mesh=mesh, in_specs=placed, out_specs=P(("shots", "src"), None, None), check_vma=False
    )
```

time: 416 us -> 267 us (0.64); the launches traced: 408 us -> 265 us
  Pallas kernels: 0 us -> 118 us
  matrix products: 111 us -> 0 us
  local copies, waits for them, and re-layouts: 96.8 us -> 10.3 us
  blocking collectives: 97 us -> 52.2 us
  other arithmetic: 39.5 us -> 16 us
  starting transfers between devices: 6.56 us -> 16.4 us
  waiting for transfers between devices: 57 us -> 52.5 us
    pallas_call x0 -> x4, Pallas kernels: none -> 118 us  [apply_levels(): pl.pallas_call(kernel, out_shape=jax.ShapeDtypeStruct((count, rows, width...]
    dot_general x16 -> x0, matrix products: 111 us -> none  [the longest x8 66.1 us: apply_level(): jnp.einsum('bij,bjk->bik', mats[:, 1], other, precision=lax.Precision.HIG...]
    all_to_all x1, blocking collectives: 97 us -> 52.2 us  [body(): lax.all_to_all(current, 'src', split_axis=0, concat_axis=0, tiled=True)]
    rev x8 -> x0, local copies, waits for them, and re-layouts: 37.2 us -> none  [pair_flip(): return jnp.flip(shaped, 1).reshape(field.shape)]
    gather x16 -> x4, local copies, waits for them, and re-layouts: 34.3 us -> 1.31 us  [the longest x2 0.66 us: body(): local_pidx = jnp.take(pattern_index[:first_cross], own_boxes, axis=1)]
    all_to_all x1 -> x2, waiting for transfers between devices: 57 us -> 34.5 us  [body(): lax.all_to_all(state, 'src', split_axis=0, concat_axis=0, tiled=True)]
    all_to_all x0 -> x1, waiting for transfers between devices: none -> 17.9 us  [body(): lax.all_to_all(current, 'src', split_axis=0, concat_axis=0, tiled=True)]
    select_n x10 -> x4, other arithmetic: 15.3 us -> 1.16 us  [the longest x2 0.6 us: body(): local_pidx = jnp.take(pattern_index[:first_cross], own_boxes, axis=1)]
  transfers between devices with their start and end apart: 1 -> 3, of which waited for: 1 -> 3; matrix products, arithmetic and copies ran while one was open for 9% -> 1% of each run, Pallas kernels for 0% -> 33%
where the time goes in v1:
time: 267 us; the launch traced here: 265 us
  Pallas kernels  118 us (44%)
  waiting for transfers between devices  52.5 us (20%)
  blocking collectives  52.2 us (20%)
  starting transfers between devices  16.4 us (6%)
  other arithmetic  16 us (6%)
  local copies, waits for them, and re-layouts  10.3 us (4%)
    pallas_call x4, Pallas kernels, apply_levels(): pl.pallas_call(kernel, out_shape=jax.ShapeDtypeStruct((count, rows, width...  118 us
    all_to_all x1, blocking collectives, body(): lax.all_to_all(current, 'src', split_axis=0, concat_axis=0, tiled=True)  52.2 us
    all_to_all x2, waiting for transfers between devices, body(): lax.all_to_all(state, 'src', split_axis=0, concat_axis=0, tiled=True)  34.5 us
    all_to_all x1, waiting for transfers between devices, body(): lax.all_to_all(current, 'src', split_axis=0, concat_axis=0, tiled=True)  17.9 us
    all_to_all x2, starting transfers between devices, body(): lax.all_to_all(state, 'src', split_axis=0, concat_axis=0, tiled=True)  11.5 us
    concatenate x1, other arithmetic, block_real_table(): return jnp.concatenate([upper, lower], axis=-2)  7.31 us
  transfers between devices with their start and end apart: 3, of which 3 were waited for; matrix products, arithmetic and copies ran while one was open for 1% of the time, Pallas kernels for 33%

profile of v1, /device:TPU:15, one launch (start us, length us, event | category | flops | bytes accessed | tf_op | source)
XLA Modules:
  0.0 265.4 jit_solution(474168927136853638)
XLA Ops:
  0.0 5.2 %fusion.3 = f32[8,8,2,64,64]{4,3,2,1,0:T(8,128)} fusion(f32[8,8,2,2,64,64]{5,4,3,2,1,0:T(8,128)} %param.6), kind=kLoop, calls=%fused_computation.22 | loop fusion | flops 524288 | bytes 4194304 | tf_op jit(solution)/shard_map/neg | solution.py:17
  5.2 0.5 copy-done
  5.7 4.2 %slice_bitcast_fusion = (f32[8,8,2,64,64]{4,3,2,1,0:T(8,128)}, f32[8,8,2,64,64]{4,3,2,1,0:T(8,128)}) fusion(f32[8,8,2,2,64,64]{5,4,3,2,1,0:T(8,128)S(1)} %copy-done), kind=kLoop, calls=%fused_computation.4 | loop fusion | bytes 8388608 | tf_op jit(solution)/shard_map/squeeze | solution.py:16
  10.0 0.1 copy.8
  10.1 0.6 gather_fusion.1
  10.7 0.1 copy.9
  10.8 7.3 %maximum_maximum_fusion = f32[8,8,2,128,128]{4,3,2,1,0:T(8,128)S(1)} fusion(f32[8,8,2,64,64]{4,3,2,1,0:T(8,128)} %get-tuple-element.9, f32[8,8,2,64,64]{4,3,2,1,0:T(8,128)} %get-tuple-element.8, f32[8,8,2,64,64]{4,3,2,1,0:T(8,128)} %fusion.3), kind=kLoop, calls=%fused_computation.2 | loop fusion | flops 6291456 | bytes 14680064 | tf_op jit(solution)/shard_map/concatenate | solution.py:19
  18.1 3.9 %fusion.4 = (f32[4,8,2,128,128]{4,3,2,1,0:T(8,128)}, f32[4,8,2,128,128]{4,3,2,1,0:T(8,128)}) fusion(f32[8,8,2,128,128]{4,3,2,1,0:T(8,128)S(1)} %maximum_maximum_fusion), kind=kLoop, calls=%fused_computation.23 | loop fusion | bytes 16777216 | tf_op jit(solution)/shard_map/slice | solution.py:101
  22.0 0.6 select_bitcast_fusion.pidx_ref
  22.6 29.5 %shard_map.37 = f32[32,128,128]{2,1,0:T(8,128)} custom-call(s32[4,32]{1,0:T(4,128)} %select_bitcast_fusion.pidx_ref, f32[4,8,2,128,128]{4,3,2,1,0:T(8,128)} %get-tuple-element.6.m_ref, f32[32,128,256]{2,1,0:T(8,128)} %x_ref.3), custom_call_target="tpu_custom_call" | custom-call | flops 1073741824 | bytes 8388608 | tf_op jit(solution)/shard_map/pallas_call | solution.py:56
  52.1 6.6 %all-to-all-start = ((f32[32,128,128]{2,1,0:T(8,128)}), f32[32,128,128]{2,1,0:T(8,128)S(1)}, u32[]{:S(2)}, u32[]{:S(2)}) async-start(f32[32,128,128]{2,1,0:T(8,128)} %shard_map.37), calls=%async_computation | async-start | bytes 4194304 | tf_op jit(solution)/shard_map/all_to_all | solution.py:106
  58.6 29.5 %shard_map.39 = f32[32,128,128]{2,1,0:T(8,128)} custom-call(s32[4,32]{1,0:T(4,128)} %select_bitcast_fusion.pidx_ref, f32[4,8,2,128,128]{4,3,2,1,0:T(8,128)} %get-tuple-element.6.m_ref, f32[32,128,256]{2,1,0:T(8,128)} %x_ref.3), custom_call_target="tpu_custom_call" | custom-call | flops 1073741824 | bytes 8388608 | tf_op jit(solution)/shard_map/pallas_call | solution.py:56
  88.1 17.9 %all-to-all-done.x_ref = f32[32,128,128]{2,1,0:T(8,128)S(1)} async-done(((f32[32,128,128]{2,1,0:T(8,128)}), f32[32,128,128]{2,1,0:T(8,128)S(1)}, u32[]{:S(2)}, u32[]{:S(2)}) %all-to-all-start) | async-done | bytes 2097184 | tf_op jit(solution)/shard_map/all_to_all | solution.py:106
  106.1 4.9 %all-to-all-start.2 = ((f32[32,128,128]{2,1,0:T(8,128)}), f32[32,128,128]{2,1,0:T(8,128)}, u32[]{:S(2)}, u32[]{:S(2)}) async-start(f32[32,128,128]{2,1,0:T(8,128)} %shard_map.39), calls=%async_computation.2 | async-start | bytes 4194304 | tf_op jit(solution)/shard_map/all_to_all | solution.py:106
  111.0 0.1 copy.4
  111.2 0.6 gather_fusion
  111.8 0.5 select_bitcast_fusion.1.pidx_ref
  112.4 29.5 %shard_map.38 = f32[32,128,128]{2,1,0:T(8,128)} custom-call(s32[4,32]{1,0:T(4,128)} %select_bitcast_fusion.1.pidx_ref, f32[4,8,2,128,128]{4,3,2,1,0:T(8,128)} %get-tuple-element.7.m_ref, f32[32,128,128]{2,1,0:T(8,128)} %copy-done.1), custom_call_target="tpu_custom_call" | custom-call | flops 1073741824 | bytes 8388608 | tf_op jit(solution)/shard_map/pallas_call | solution.py:56
  141.9 16.6 %all-to-all-done.2.x_ref = f32[32,128,128]{2,1,0:T(8,128)} async-done(((f32[32,128,128]{2,1,0:T(8,128)}), f32[32,128,128]{2,1,0:T(8,128)}, u32[]{:S(2)}, u32[]{:S(2)}) %all-to-all-start.2) | async-done | bytes 2097184 | tf_op jit(solution)/shard_map/all_to_all | solution.py:106
  158.5 4.9 %all-to-all-start.1 = ((f32[32,128,128]{2,1,0:T(8,128)}), f32[32,128,128]{2,1,0:T(8,128)S(1)}, u32[]{:S(2)}, u32[]{:S(2)}) async-start(f32[32,128,128]{2,1,0:T(8,128)} %shard_map.38), calls=%async_computation.1 | async-start | bytes 4194304 | tf_op jit(solution)/shard_map/all_to_all | solution.py:108
  163.4 29.5 %shard_map.40 = f32[32,128,128]{2,1,0:T(8,128)} custom-call(s32[4,32]{1,0:T(4,128)} %select_bitcast_fusion.1.pidx_ref, f32[4,8,2,128,128]{4,3,2,1,0:T(8,128)} %get-tuple-element.7.m_ref, f32[32,128,128]{2,1,0:T(8,128)} %all-to-all-done.2.x_ref), custom_call_target="tpu_custom_call" | custom-call | flops 1073741824 | bytes 8388608 | tf_op jit(solution)/shard_map/pallas_call | solution.py:56
  192.9 17.9 %all-to-all-done.1 = f32[32,128,128]{2,1,0:T(8,128)S(1)} async-done(((f32[32,128,128]{2,1,0:T(8,128)}), f32[32,128,128]{2,1,0:T(8,128)S(1)}, u32[]{:S(2)}, u32[]{:S(2)}) %all-to-all-start.1) | async-done | bytes 2097184 | tf_op jit(solution)/shard_map/all_to_all | solution.py:108
  210.8 52.2 %all_to_all.20 = f32[32,128,128]{2,1,0:T(8,128)S(1)} all-to-all(f32[32,128,128]{2,1,0:T(8,128)} %shard_map.40), channel_id=1, replica_groups=mesh['shots'=2,'src'=16] {'src'}, dimensions={0} | all-to-all | bytes 4194304 | tf_op jit(solution)/shard_map/all_to_all | solution.py:108
  263.0 2.3 pad_maximum_fusion
  (13 shorter events, 0.1 us)
Async XLA Ops:
  0.0 5.7 %copy-start = (f32[8,8,2,2,64,64]{5,4,3,2,1,0:T(8,128)S(1)}, f32[8,8,2,2,64,64]{5,4,3,2,1,0:T(8,128)}, u32[]{:S(2)}) copy-start(f32[8,8,2,2,64,64]{5,4,3,2,1,0:T(8,128)} %param.6) | copy-start | bytes 12582916
  5.7 4.2 %copy-start.2 = (s32[8,512]{1,0:T(8,128)S(1)}, s32[8,512]{1,0:T(8,128)}, u32[]{:S(2)}) copy-start(s32[8,512]{1,0:T(8,128)} %param.7) | copy-start | bytes 49156
  52.1 54.0 %all-to-all-start = ((f32[32,128,128]{2,1,0:T(8,128)}), f32[32,128,128]{2,1,0:T(8,128)S(1)}, u32[]{:S(2)}, u32[]{:S(2)}) async-start(f32[32,128,128]{2,1,0:T(8,128)} %shard_map.37), calls=%async_computation | async-start | bytes 4194304 | tf_op jit(solution)/shard_map/all_to_all | solution.py:106
  106.1 6.3 %copy-start.1 = (f32[32,128,128]{2,1,0:T(8,128)}, f32[32,128,128]{2,1,0:T(8,128)S(1)}, u32[]{:S(2)}) copy-start(f32[32,128,128]{2,1,0:T(8,128)S(1)} %all-to-all-done.x_ref) | copy-start | bytes 6291460
  106.1 52.4 %all-to-all-start.2 = ((f32[32,128,128]{2,1,0:T(8,128)}), f32[32,128,128]{2,1,0:T(8,128)}, u32[]{:S(2)}, u32[]{:S(2)}) async-start(f32[32,128,128]{2,1,0:T(8,128)} %shard_map.39), calls=%async_computation.2 | async-start | bytes 4194304 | tf_op jit(solution)/shard_map/all_to_all | solution.py:106
  158.5 52.3 %all-to-all-start.1 = ((f32[32,128,128]{2,1,0:T(8,128)}), f32[32,128,128]{2,1,0:T(8,128)S(1)}, u32[]{:S(2)}, u32[]{:S(2)}) async-start(f32[32,128,128]{2,1,0:T(8,128)} %shard_map.38), calls=%async_computation.1 | async-start | bytes 4194304 | tf_op jit(solution)/shard_map/all_to_all | solution.py:108

commit v2 on v0

v2 whole, which is shorter than its diff:
```python
import functools

import jax
import jax.numpy as jnp
from jax import lax
from jax.experimental import pallas as pl
from jax.experimental.pallas import tpu as pltpu
from jax.sharding import PartitionSpec as P

LEVELS = 8
K_CHUNKS = 2
PARITY_SPLIT = True


def levels_kernel(masks, pidx_ref, tr_ref, x_ref, o_ref, table, buf):
    level = pl.program_id(0)
    patterns = tr_ref.shape[1]
    rank = tr_ref.shape[4]
    for p in range(patterns):
        for j in range(2):
            re = tr_ref[0, p, j, 0]
            im = tr_ref[0, p, j, 1]
            table[p, j, 0:rank] = re - pltpu.roll(im, rank, 1)
            table[p, j, rank : 2 * rank] = im + pltpu.roll(re, rank, 1)

    count = x_ref.shape[0]
    last = len(masks) - 1
    for li, mask in enumerate(masks):
        src = x_ref if li == 0 else buf.at[(li - 1) % 2]
        dst = o_ref if li == last else buf.at[li % 2]

        @pl.when(level == li)
        def _(src=src, dst=dst, li=li, mask=mask):
            def pair(i, carry):
                lo = (i // mask) * (2 * mask) + i % mask
                hi = lo + mask
                p_lo = pidx_ref[li, lo]
                p_hi = pidx_ref[li, hi]
                lhs = jnp.concatenate(
                    [
                        jnp.concatenate([table[p_lo, 0], table[p_lo, 1]], axis=1),
                        jnp.concatenate([table[p_hi, 1], table[p_hi, 0]], axis=1),
                    ],
                    axis=0,
                )
                rhs = jnp.concatenate([src[lo], src[hi]], axis=0)
                out = jnp.dot(lhs, rhs, precision=lax.Precision.HIGHEST, preferred_element_type=jnp.float32)
                half = out.shape[0] // 2
                dst[lo] = out[:half]
                dst[hi] = out[half:]
                return carry

            lax.fori_loop(0, count // 2, pair, 0)


def apply_levels(state, trp, pidx, masks, level_offset, index_of, count, width):
    rows = state.shape[-2]
    n_levels = len(masks)
    patterns = trp.shape[1]
    rank = trp.shape[4]
    block = (count, None, rows, width) if state.ndim == 4 else (count, rows, width)
    flops = 2 * count * rows * 2 * rows * width * n_levels
    return pl.pallas_call(
        functools.partial(levels_kernel, tuple(masks)),
        out_shape=jax.ShapeDtypeStruct((count, rows, width), state.dtype),
        grid_spec=pltpu.PrefetchScalarGridSpec(
            num_scalar_prefetch=1,
            grid=(n_levels,),
            in_specs=[
                pl.BlockSpec((1,) + trp.shape[1:], lambda i, p: (level_offset + i, 0, 0, 0, 0, 0)),
                pl.BlockSpec(block, lambda i, p: index_of),
            ],
            out_specs=pl.BlockSpec((count, rows, width), lambda i, p: (0, 0, 0)),
            scratch_shapes=[
                pltpu.VMEM((patterns, 2, 2 * rank, 2 * rank), jnp.float32),
                pltpu.VMEM((2, count, rows, width), jnp.float32),
            ],
        ),
        compiler_params=pltpu.CompilerParams(vmem_limit_bytes=48 * 1024 * 1024),
        cost_estimate=pl.CostEstimate(
            flops=flops, transcendentals=0, bytes_accessed=2 * count * rows * width * 4 + n_levels * trp[0].size * 4
        ),
    )(pidx, trp, state)


def body(weights_in, translations, pattern_index):
    box_count, rows, k_len = weights_in.shape
    groups = lax.axis_size("src")
    local_bits = box_count.bit_length() - 1
    top_bits = (box_count * groups).bit_length() - 1
    device = lax.axis_index("src")
    rank = translations.shape[-1]
    trp = jnp.pad(translations, [(0, 0)] * 5 + [(0, rank)])
    bits = [top_bits - LEVELS + level for level in range(LEVELS)]
    first_cross = next((lv for lv, b in enumerate(bits) if b >= local_bits), LEVELS)

    split = 2 if (PARITY_SPLIT and bits[0] >= 1 and box_count // 2 >= groups) else 1
    split_bits = split.bit_length() - 1
    count = box_count // split
    repeat = count // groups
    repeat_bits = repeat.bit_length() - 1
    width = k_len // K_CHUNKS
    shaped = weights_in.reshape(count, split, rows, k_len) if split > 1 else weights_in

    slot = jnp.arange(count, dtype=jnp.int32)
    local_masks = [1 << (bits[lv] - split_bits) for lv in range(first_cross)]
    cross_masks = [1 << (bits[lv] - local_bits + repeat_bits) for lv in range(first_cross, LEVELS)]

    pieces = {}
    for parity in range(split):
        own_boxes = device * box_count + slot * split + parity
        held_boxes = slot // repeat * box_count + (device * repeat + slot % repeat) * split + parity
        local_pidx = jnp.take(pattern_index[:first_cross], own_boxes, axis=1)
        cross_pidx = jnp.take(pattern_index[first_cross:], held_boxes, axis=1)
        for chunk in range(K_CHUNKS):
            index_of = (0, parity, 0, chunk) if split > 1 else (0, 0, chunk)
            if first_cross > 0:
                state = apply_levels(shaped, trp, local_pidx, local_masks, 0, index_of, count, width)
            elif split > 1:
                state = shaped[:, parity, :, chunk * width : (chunk + 1) * width]
            else:
                state = shaped[:, :, chunk * width : (chunk + 1) * width]
            current = lax.all_to_all(state, "src", split_axis=0, concat_axis=0, tiled=True)
            current = apply_levels(
                current, trp, cross_pidx, cross_masks, first_cross, (0, 0, 0), count, width
            )
            pieces[parity, chunk] = lax.all_to_all(current, "src", split_axis=0, concat_axis=0, tiled=True)
    joined = [jnp.concatenate([pieces[parity, c] for c in range(K_CHUNKS)], axis=-1) for parity in range(split)]
    if split > 1:
        return jnp.stack(joined, axis=1).reshape(box_count, rows, k_len)
    return joined[0]


def solution(mesh):
    placed = (P(("shots", "src"), None, None), P(), P())
    return jax.shard_map(
        body, mesh=mesh, in_specs=placed, out_specs=P(("shots", "src"), None, None), check_vma=False
    )
```

time: 416 us -> 273 us (0.66); the launches traced: 408 us -> 272 us
  Pallas kernels: 0 us -> 130 us
  matrix products: 111 us -> 0 us
  blocking collectives: 97 us -> 0 us
  local copies, waits for them, and re-layouts: 96.8 us -> 23.3 us
  other arithmetic: 39.5 us -> 3.59 us
  starting transfers between devices: 6.56 us -> 41.1 us
  waiting for transfers between devices: 57 us -> 73.5 us
    pallas_call x0 -> x8, Pallas kernels: none -> 130 us  [apply_levels(): pl.pallas_call(functools.partial(levels_kernel, tuple(masks)), out_shape=...]
    dot_general x16 -> x0, matrix products: 111 us -> none  [the longest x8 66.1 us: apply_level(): jnp.einsum('bij,bjk->bik', mats[:, 1], other, precision=lax.Precision.HIG...]
    all_to_all x1 -> x0, blocking collectives: 97 us -> none  [body(): lax.all_to_all(current, 'src', split_axis=0, concat_axis=0, tiled=True)]
    all_to_all x0 -> x4, waiting for transfers between devices: none -> 48.3 us  [body(): lax.all_to_all(current, 'src', split_axis=0, concat_axis=0, tiled=True)]
    rev x8 -> x0, local copies, waits for them, and re-layouts: 37.2 us -> none  [pair_flip(): return jnp.flip(shaped, 1).reshape(field.shape)]
    all_to_all x1 -> x4, waiting for transfers between devices: 57 us -> 25.2 us  [body(): lax.all_to_all(state, 'src', split_axis=0, concat_axis=0, tiled=True)]
    gather x16 -> x8, local copies, waits for them, and re-layouts: 34.3 us -> 2.58 us  [the longest x4 1.29 us: body(): local_pidx = jnp.take(pattern_index[:first_cross], own_boxes, axis=1)]
    all_to_all x0 -> x4, starting transfers between devices: none -> 19.8 us  [body(): lax.all_to_all(current, 'src', split_axis=0, concat_axis=0, tiled=True)]
  transfers between devices with their start and end apart: 1 -> 8, of which waited for: 1 -> 8; matrix products, arithmetic and copies ran while one was open for 9% -> 1% of each run, Pallas kernels for 0% -> 42%
where the time goes in v2:
time: 273 us; the launch traced here: 272 us
  Pallas kernels  130 us (48%)
  waiting for transfers between devices  73.5 us (27%)
  starting transfers between devices  41.1 us (15%)
  local copies, waits for them, and re-layouts  23.3 us (9%)
  other arithmetic  3.59 us (1%)
    pallas_call x8, Pallas kernels, apply_levels(): pl.pallas_call(functools.partial(levels_kernel, tuple(masks)), out_shape=...  130 us
    all_to_all x4, waiting for transfers between devices, body(): lax.all_to_all(current, 'src', split_axis=0, concat_axis=0, tiled=True)  48.3 us
    all_to_all x4, waiting for transfers between devices, body(): lax.all_to_all(state, 'src', split_axis=0, concat_axis=0, tiled=True)  25.2 us
    all_to_all x4, starting transfers between devices, body(): lax.all_to_all(state, 'src', split_axis=0, concat_axis=0, tiled=True)  21.4 us
    all_to_all x4, starting transfers between devices, body(): lax.all_to_all(current, 'src', split_axis=0, concat_axis=0, tiled=True)  19.8 us
    unnamed x18, local copies, waits for them, and re-layouts  8.81 us
    pad x1, local copies, waits for them, and re-layouts, body(): trp = jnp.pad(translations, [(0, 0)] * 5 + [(0, rank)])  8.71 us
  transfers between devices with their start and end apart: 8, of which 8 were waited for; matrix products, arithmetic and copies ran while one was open for 1% of the time, Pallas kernels for 42%

profile of v2, /device:TPU:15, one launch (start us, length us, event | category | flops | bytes accessed | tf_op | source)
XLA Modules:
  0.0 271.8 jit_solution(1953033453315198450)
XLA Ops:
  1.6 8.7 %pad.4.tr_ref = f32[8,8,2,2,64,128]{5,4,3,2,1,0:T(8,128)} pad(f32[8,8,2,2,64,64]{5,4,3,2,1,0:T(8,128)} %param.6, f32[]{:T(128)} %constant.50.clone.1), padding=0_0x0_0x0_0x0_0x0_0x0_64 | pad | bytes 12582916 | tf_op jit(solution)/shard_map/jit(_pad)/pad | solution.py:93
  10.4 16.5 %shard_map.43 = f32[16,128,128]{2,1,0:T(8,128)} custom-call(s32[4,16]{1,0:T(4,128)S(1)} %select_bitcast_fusion.pidx_ref, f32[8,8,2,2,64,128]{5,4,3,2,1,0:T(8,128)} %pad.4.tr_ref, f32[16,2,128,256]{3,2,1,0:T(8,128)S(1)} %bitcast.14), custom_call_target="tpu_custom_call" | custom-call | flops 536870912 | bytes 6291456 | tf_op jit(solution)/shard_map/pallas_call | solution.py:63
  26.9 6.6 %all-to-all-start.6 = ((f32[16,128,128]{2,1,0:T(8,128)}), f32[16,128,128]{2,1,0:T(8,128)S(1)}, u32[]{:S(2)}, u32[]{:S(2)}) async-start(f32[16,128,128]{2,1,0:T(8,128)} %shard_map.43), calls=%async_computation.6 | async-start | bytes 2097152 | tf_op jit(solution)/shard_map/all_to_all | solution.py:123
  35.6 16.6 %shard_map.41 = f32[16,128,128]{2,1,0:T(8,128)} custom-call(s32[4,16]{1,0:T(4,128)S(1)} %select_bitcast_fusion.pidx_ref, f32[8,8,2,2,64,128]{5,4,3,2,1,0:T(8,128)} %pad.4.tr_ref, f32[16,2,128,256]{3,2,1,0:T(8,128)S(1)} %bitcast.15), custom_call_target="tpu_custom_call" | custom-call | flops 536870912 | bytes 6291456 | tf_op jit(solution)/shard_map/pallas_call | solution.py:63
  52.2 6.1 %all-to-all-done.6.x_ref = f32[16,128,128]{2,1,0:T(8,128)S(1)} async-done(((f32[16,128,128]{2,1,0:T(8,128)}), f32[16,128,128]{2,1,0:T(8,128)S(1)}, u32[]{:S(2)}, u32[]{:S(2)}) %all-to-all-start.6) | async-done | bytes 1048608 | tf_op jit(solution)/shard_map/all_to_all | solution.py:123
  58.3 4.9 %all-to-all-start.4 = ((f32[16,128,128]{2,1,0:T(8,128)}), f32[16,128,128]{2,1,0:T(8,128)S(1)}, u32[]{:S(2)}, u32[]{:S(2)}) async-start(f32[16,128,128]{2,1,0:T(8,128)} %shard_map.41), calls=%async_computation.4 | async-start | bytes 2097152 | tf_op jit(solution)/shard_map/all_to_all | solution.py:123
  66.1 16.5 %shard_map.39 = f32[16,128,128]{2,1,0:T(8,128)} custom-call(s32[4,16]{1,0:T(4,128)S(1)} %select_bitcast_fusion.2.pidx_ref, f32[8,8,2,2,64,128]{5,4,3,2,1,0:T(8,128)} %pad.4.tr_ref, f32[16,2,128,256]{3,2,1,0:T(8,128)S(1)} %bitcast.16), custom_call_target="tpu_custom_call" | custom-call | flops 536870912 | bytes 6291456 | tf_op jit(solution)/shard_map/pallas_call | solution.py:63
  82.6 5.5 %all-to-all-done.4.x_ref = f32[16,128,128]{2,1,0:T(8,128)S(1)} async-done(((f32[16,128,128]{2,1,0:T(8,128)}), f32[16,128,128]{2,1,0:T(8,128)S(1)}, u32[]{:S(2)}, u32[]{:S(2)}) %all-to-all-start.4) | async-done | bytes 1048608 | tf_op jit(solution)/shard_map/all_to_all | solution.py:123
  88.1 4.9 %all-to-all-start.2 = ((f32[16,128,128]{2,1,0:T(8,128)}), f32[16,128,128]{2,1,0:T(8,128)S(1)}, u32[]{:S(2)}, u32[]{:S(2)}) async-start(f32[16,128,128]{2,1,0:T(8,128)} %shard_map.39), calls=%async_computation.2 | async-start | bytes 2097152 | tf_op jit(solution)/shard_map/all_to_all | solution.py:123
  95.2 16.6 %shard_map.37 = f32[16,128,128]{2,1,0:T(8,128)} custom-call(s32[4,16]{1,0:T(4,128)S(1)} %select_bitcast_fusion.2.pidx_ref, f32[8,8,2,2,64,128]{5,4,3,2,1,0:T(8,128)} %pad.4.tr_ref, f32[16,2,128,256]{3,2,1,0:T(8,128)S(1)} %bitcast.17), custom_call_target="tpu_custom_call" | custom-call | flops 536870912 | bytes 6291456 | tf_op jit(solution)/shard_map/pallas_call | solution.py:63
  111.8 6.1 %all-to-all-done.2.x_ref = f32[16,128,128]{2,1,0:T(8,128)S(1)} async-done(((f32[16,128,128]{2,1,0:T(8,128)}), f32[16,128,128]{2,1,0:T(8,128)S(1)}, u32[]{:S(2)}, u32[]{:S(2)}) %all-to-all-start.2) | async-done | bytes 1048608 | tf_op jit(solution)/shard_map/all_to_all | solution.py:123
  117.9 4.9 %all-to-all-start = ((f32[16,128,128]{2,1,0:T(8,128)}), f32[16,128,128]{2,1,0:T(8,128)S(1)}, u32[]{:S(2)}, u32[]{:S(2)}) async-start(f32[16,128,128]{2,1,0:T(8,128)} %shard_map.37), calls=%async_computation | async-start | bytes 2097152 | tf_op jit(solution)/shard_map/all_to_all | solution.py:123
  123.7 15.5 %shard_map.44 = f32[16,128,128]{2,1,0:T(8,128)S(1)} custom-call(s32[4,16]{1,0:T(4,128)S(1)} %select_bitcast_fusion.1.pidx_ref, f32[8,8,2,2,64,128]{5,4,3,2,1,0:T(8,128)} %pad.4.tr_ref, f32[16,128,128]{2,1,0:T(8,128)S(1)} %all-to-all-done.6.x_ref), custom_call_target="tpu_custom_call" | custom-call | flops 536870912 | bytes 6291456 | tf_op jit(solution)/shard_map/pallas_call | solution.py:63
  140.2 7.5 %all-to-all-done.x_ref = f32[16,128,128]{2,1,0:T(8,128)S(1)} async-done(((f32[16,128,128]{2,1,0:T(8,128)}), f32[16,128,128]{2,1,0:T(8,128)S(1)}, u32[]{:S(2)}, u32[]{:S(2)}) %all-to-all-start) | async-done | bytes 1048608 | tf_op jit(solution)/shard_map/all_to_all | solution.py:123
  147.7 4.9 %all-to-all-start.7 = ((f32[16,128,128]{2,1,0:T(8,128)}), f32[16,128,128]{2,1,0:T(8,128)}, u32[]{:S(2)}, u32[]{:S(2)}) async-start(f32[16,128,128]{2,1,0:T(8,128)} %copy-done.7), calls=%async_computation.7 | async-start | bytes 2097152 | tf_op jit(solution)/shard_map/all_to_all | solution.py:127
  152.7 15.5 %shard_map.42 = f32[16,128,128]{2,1,0:T(8,128)S(1)} custom-call(s32[4,16]{1,0:T(4,128)S(1)} %select_bitcast_fusion.1.pidx_ref, f32[8,8,2,2,64,128]{5,4,3,2,1,0:T(8,128)} %pad.4.tr_ref, f32[16,128,128]{2,1,0:T(8,128)S(1)} %copy-done.5), custom_call_target="tpu_custom_call" | custom-call | flops 536870912 | bytes 6291456 | tf_op jit(solution)/shard_map/pallas_call | solution.py:63
  169.2 8.4 %all-to-all-done.7 = f32[16,128,128]{2,1,0:T(8,128)} async-done(((f32[16,128,128]{2,1,0:T(8,128)}), f32[16,128,128]{2,1,0:T(8,128)}, u32[]{:S(2)}, u32[]{:S(2)}) %all-to-all-start.7) | async-done | bytes 1048608 | tf_op jit(solution)/shard_map/all_to_all | solution.py:127
  177.7 4.9 %all-to-all-start.5 = ((f32[16,128,128]{2,1,0:T(8,128)}), f32[16,128,128]{2,1,0:T(8,128)S(1)}, u32[]{:S(2)}, u32[]{:S(2)}) async-start(f32[16,128,128]{2,1,0:T(8,128)} %copy-done.6), calls=%async_computation.5 | async-start | bytes 2097152 | tf_op jit(solution)/shard_map/all_to_all | solution.py:127
  183.3 16.5 %shard_map.40 = f32[16,128,128]{2,1,0:T(8,128)} custom-call(s32[4,16]{1,0:T(4,128)S(1)} %select_bitcast_fusion.3.pidx_ref, f32[8,8,2,2,64,128]{5,4,3,2,1,0:T(8,128)} %pad.4.tr_ref, f32[16,128,128]{2,1,0:T(8,128)S(1)} %all-to-all-done.2.x_ref), custom_call_target="tpu_custom_call" | custom-call | flops 536870912 | bytes 6291456 | tf_op jit(solution)/shard_map/pallas_call | solution.py:63
  199.8 7.7 %all-to-all-done.5 = f32[16,128,128]{2,1,0:T(8,128)S(1)} async-done(((f32[16,128,128]{2,1,0:T(8,128)}), f32[16,128,128]{2,1,0:T(8,128)S(1)}, u32[]{:S(2)}, u32[]{:S(2)}) %all-to-all-start.5) | async-done | bytes 1048608 | tf_op jit(solution)/shard_map/all_to_all | solution.py:127
  207.5 4.9 %all-to-all-start.3 = ((f32[16,128,128]{2,1,0:T(8,128)}), f32[16,128,128]{2,1,0:T(8,128)}, u32[]{:S(2)}, u32[]{:S(2)}) async-start(f32[16,128,128]{2,1,0:T(8,128)} %shard_map.40), calls=%async_computation.3 | async-start | bytes 2097152 | tf_op jit(solution)/shard_map/all_to_all | solution.py:127
  212.4 16.5 %shard_map.38 = f32[16,128,128]{2,1,0:T(8,128)} custom-call(s32[4,16]{1,0:T(4,128)S(1)} %select_bitcast_fusion.3.pidx_ref, f32[8,8,2,2,64,128]{5,4,3,2,1,0:T(8,128)} %pad.4.tr_ref, f32[16,128,128]{2,1,0:T(8,128)S(1)} %all-to-all-done.x_ref), custom_call_target="tpu_custom_call" | custom-call | flops 536870912 | bytes 6291456 | tf_op jit(solution)/shard_map/pallas_call | solution.py:63
  228.9 8.5 %all-to-all-done.3 = f32[16,128,128]{2,1,0:T(8,128)} async-done(((f32[16,128,128]{2,1,0:T(8,128)}), f32[16,128,128]{2,1,0:T(8,128)}, u32[]{:S(2)}, u32[]{:S(2)}) %all-to-all-start.3) | async-done | bytes 1048608 | tf_op jit(solution)/shard_map/all_to_all | solution.py:127
  243.7 23.6 %all-to-all-done.1 = f32[16,128,128]{2,1,0:T(8,128)} async-done(((f32[16,128,128]{2,1,0:T(8,128)}), f32[16,128,128]{2,1,0:T(8,128)}, u32[]{:S(2)}, u32[]{:S(2)}) %all-to-all-start.1) | async-done | bytes 1048608 | tf_op jit(solution)/shard_map/all_to_all | solution.py:127
  (45 shorter events, 23.1 us)
Async XLA Ops:
  1.6 8.7 %copy-start = (f32[32,128,256]{2,1,0:T(8,128)S(1)}, f32[32,128,256]{2,1,0:T(8,128)}, u32[]{:S(2)}) copy-start(f32[32,128,256]{2,1,0:T(8,128)} %param.5) | copy-start | bytes 12582916
  26.9 31.4 %all-to-all-start.6 = ((f32[16,128,128]{2,1,0:T(8,128)}), f32[16,128,128]{2,1,0:T(8,128)S(1)}, u32[]{:S(2)}, u32[]{:S(2)}) async-start(f32[16,128,128]{2,1,0:T(8,128)} %shard_map.43), calls=%async_computation.6 | async-start | bytes 2097152 | tf_op jit(solution)/shard_map/all_to_all | solution.py:123
  33.4 2.2 copy-start.1
  58.3 29.8 %all-to-all-start.4 = ((f32[16,128,128]{2,1,0:T(8,128)}), f32[16,128,128]{2,1,0:T(8,128)S(1)}, u32[]{:S(2)}, u32[]{:S(2)}) async-start(f32[16,128,128]{2,1,0:T(8,128)} %shard_map.41), calls=%async_computation.4 | async-start | bytes 2097152 | tf_op jit(solution)/shard_map/all_to_all | solution.py:123
  63.9 2.2 copy-start.2
  88.1 23.7 %copy-start.4 = (f32[16,128,128]{2,1,0:T(8,128)}, f32[16,128,128]{2,1,0:T(8,128)S(1)}, u32[]{:S(2)}) copy-start(f32[16,128,128]{2,1,0:T(8,128)S(1)} %all-to-all-done.4.x_ref) | copy-start | bytes 3145732
  88.1 29.8 %all-to-all-start.2 = ((f32[16,128,128]{2,1,0:T(8,128)}), f32[16,128,128]{2,1,0:T(8,128)S(1)}, u32[]{:S(2)}, u32[]{:S(2)}) async-start(f32[16,128,128]{2,1,0:T(8,128)} %shard_map.39), calls=%async_computation.2 | async-start | bytes 2097152 | tf_op jit(solution)/shard_map/all_to_all | solution.py:123
  93.1 2.2 copy-start.3
  117.9 29.8 %all-to-all-start = ((f32[16,128,128]{2,1,0:T(8,128)}), f32[16,128,128]{2,1,0:T(8,128)S(1)}, u32[]{:S(2)}, u32[]{:S(2)}) async-start(f32[16,128,128]{2,1,0:T(8,128)} %shard_map.37), calls=%async_computation | async-start | bytes 2097152 | tf_op jit(solution)/shard_map/all_to_all | solution.py:123
  139.2 1.0 copy-start.7
  140.2 12.5 %copy-start.5 = (f32[16,128,128]{2,1,0:T(8,128)S(1)}, f32[16,128,128]{2,1,0:T(8,128)}, u32[]{:S(2)}) copy-start(f32[16,128,128]{2,1,0:T(8,128)} %copy-done.4) | copy-start | bytes 3145732
  147.7 29.9 %all-to-all-start.7 = ((f32[16,128,128]{2,1,0:T(8,128)}), f32[16,128,128]{2,1,0:T(8,128)}, u32[]{:S(2)}, u32[]{:S(2)}) async-start(f32[16,128,128]{2,1,0:T(8,128)} %copy-done.7), calls=%async_computation.7 | async-start | bytes 2097152 | tf_op jit(solution)/shard_map/all_to_all | solution.py:127
  168.2 1.0 copy-start.6
  177.7 29.8 %all-to-all-start.5 = ((f32[16,128,128]{2,1,0:T(8,128)}), f32[16,128,128]{2,1,0:T(8,128)S(1)}, u32[]{:S(2)}, u32[]{:S(2)}) async-start(f32[16,128,128]{2,1,0:T(8,128)} %copy-done.6), calls=%async_computation.5 | async-start | bytes 2097152 | tf_op jit(solution)/shard_map/all_to_all | solution.py:127
  207.5 29.9 %all-to-all-start.3 = ((f32[16,128,128]{2,1,0:T(8,128)}), f32[16,128,128]{2,1,0:T(8,128)}, u32[]{:S(2)}, u32[]{:S(2)}) async-start(f32[16,128,128]{2,1,0:T(8,128)} %shard_map.40), calls=%async_computation.3 | async-start | bytes 2097152 | tf_op jit(solution)/shard_map/all_to_all | solution.py:127
  237.4 29.9 %all-to-all-start.1 = ((f32[16,128,128]{2,1,0:T(8,128)}), f32[16,128,128]{2,1,0:T(8,128)}, u32[]{:S(2)}, u32[]{:S(2)}) async-start(f32[16,128,128]{2,1,0:T(8,128)} %shard_map.38), calls=%async_computation.1 | async-start | bytes 2097152 | tf_op jit(solution)/shard_map/all_to_all | solution.py:127

commit v3 on v2

--- a/solution.py
+++ b/solution.py
@@ -15,13 +15,13 @@
 def levels_kernel(masks, pidx_ref, tr_ref, x_ref, o_ref, table, buf):
     level = pl.program_id(0)
     patterns = tr_ref.shape[1]
-    rank = tr_ref.shape[4]
+    rank = tr_ref.shape[-1]
     for p in range(patterns):
         for j in range(2):
             re = tr_ref[0, p, j, 0]
             im = tr_ref[0, p, j, 1]
-            table[p, j, 0:rank] = re - pltpu.roll(im, rank, 1)
-            table[p, j, rank : 2 * rank] = im + pltpu.roll(re, rank, 1)
+            table[p, j, 0:rank] = jnp.concatenate([re, -im], axis=1)
+            table[p, j, rank : 2 * rank] = jnp.concatenate([im, re], axis=1)
 
     count = x_ref.shape[0]
     last = len(masks) - 1
@@ -57,7 +57,7 @@
     rows = state.shape[-2]
     n_levels = len(masks)
     patterns = trp.shape[1]
-    rank = trp.shape[4]
+    rank = trp.shape[-1]
     block = (count, None, rows, width) if state.ndim == 4 else (count, rows, width)
     flops = 2 * count * rows * 2 * rows * width * n_levels
     return pl.pallas_call(
@@ -89,8 +89,6 @@
     local_bits = box_count.bit_length() - 1
     top_bits = (box_count * groups).bit_length() - 1
     device = lax.axis_index("src")
-    rank = translations.shape[-1]
-    trp = jnp.pad(translations, [(0, 0)] * 5 + [(0, rank)])
     bits = [top_bits - LEVELS + level for level in range(LEVELS)]
     first_cross = next((lv for lv, b in enumerate(bits) if b >= local_bits), LEVELS)
 
@@ -99,7 +97,8 @@
     count = box_count // split
     repeat = count // groups
     repeat_bits = repeat.bit_length() - 1
-    width = k_len // K_CHUNKS
+    k_chunks = 1 if split > 1 else K_CHUNKS
+    width = k_len // k_chunks
     shaped = weights_in.reshape(count, split, rows, k_len) if split > 1 else weights_in
 
     slot = jnp.arange(count, dtype=jnp.int32)
@@ -112,20 +111,20 @@
         held_boxes = slot // repeat * box_count + (device * repeat + slot % repeat) * split + parity
         local_pidx = jnp.take(pattern_index[:first_cross], own_boxes, axis=1)
         cross_pidx = jnp.take(pattern_index[first_cross:], held_boxes, axis=1)
-        for chunk in range(K_CHUNKS):
+        for chunk in range(k_chunks):
             index_of = (0, parity, 0, chunk) if split > 1 else (0, 0, chunk)
             if first_cross > 0:
-                state = apply_levels(shaped, trp, local_pidx, local_masks, 0, index_of, count, width)
+                state = apply_levels(shaped, translations, local_pidx, local_masks, 0, index_of, count, width)
             elif split > 1:
                 state = shaped[:, parity, :, chunk * width : (chunk + 1) * width]
             else:
                 state = shaped[:, :, chunk * width : (chunk + 1) * width]
             current = lax.all_to_all(state, "src", split_axis=0, concat_axis=0, tiled=True)
             current = apply_levels(
-                current, trp, cross_pidx, cross_masks, first_cross, (0, 0, 0), count, width
+                current, translations, cross_pidx, cross_masks, first_cross, (0, 0, 0), count, width
             )
             pieces[parity, chunk] = lax.all_to_all(current, "src", split_axis=0, concat_axis=0, tiled=True)
-    joined = [jnp.concatenate([pieces[parity, c] for c in range(K_CHUNKS)], axis=-1) for parity in range(split)]
+    joined = [jnp.concatenate([pieces[parity, c] for c in range(k_chunks)], axis=-1) for parity in range(split)]
     if split > 1:
         return jnp.stack(joined, axis=1).reshape(box_count, rows, k_len)
     return joined[0]

time: 273 us -> 238 us (0.87)
  Pallas kernels: 130 us -> 63.5 us
  blocking collectives: 0 us -> 52.2 us
  starting transfers between devices: 41.1 us -> 16.4 us
  waiting for transfers between devices: 73.5 us -> 87.4 us
  local copies, waits for them, and re-layouts: 23.3 us -> 14.2 us
    pallas_call x8 -> x4, Pallas kernels: 130 us -> 63.5 us  [apply_levels(): pl.pallas_call(functools.partial(levels_kernel, tuple(masks)), out_shape=...]
    all_to_all x0 -> x1, blocking collectives: none -> 52.2 us  [body(): lax.all_to_all(current, 'src', split_axis=0, concat_axis=0, tiled=True)]
    all_to_all x4 -> x2, waiting for transfers between devices: 25.2 us -> 57.4 us  [body(): lax.all_to_all(state, 'src', split_axis=0, concat_axis=0, tiled=True)]
    all_to_all x4 -> x1, waiting for transfers between devices: 48.3 us -> 30 us  [body(): lax.all_to_all(current, 'src', split_axis=0, concat_axis=0, tiled=True)]
    all_to_all x4 -> x1, starting transfers between devices: 19.8 us -> 4.91 us  [body(): lax.all_to_all(current, 'src', split_axis=0, concat_axis=0, tiled=True)]
    all_to_all x4 -> x2, starting transfers between devices: 21.4 us -> 11.5 us  [body(): lax.all_to_all(state, 'src', split_axis=0, concat_axis=0, tiled=True)]
    pad x1 -> x0, local copies, waits for them, and re-layouts: 8.71 us -> none  [body(): trp = jnp.pad(translations, [(0, 0)] * 5 + [(0, rank)])]
    unnamed x18 -> x14, local copies, waits for them, and re-layouts: 8.81 us -> 8.47 us
  transfers between devices with their start and end apart: 8 -> 3, of which waited for: 8 -> 3; matrix products, arithmetic and copies ran while one was open for 1% -> 1% of each run, Pallas kernels for 42% -> 20%
where the time goes in v3:
time: 238 us; the launch traced here: 236 us
  waiting for transfers between devices  87.4 us (37%)
  Pallas kernels  63.5 us (27%)
  blocking collectives  52.2 us (22%)
  starting transfers between devices  16.4 us (7%)
  local copies, waits for them, and re-layouts  14.2 us (6%)
    pallas_call x4, Pallas kernels, apply_levels(): pl.pallas_call(functools.partial(levels_kernel, tuple(masks)), out_shape=...  63.5 us
    all_to_all x2, waiting for transfers between devices, body(): lax.all_to_all(state, 'src', split_axis=0, concat_axis=0, tiled=True)  57.4 us
    all_to_all x1, blocking collectives, body(): lax.all_to_all(current, 'src', split_axis=0, concat_axis=0, tiled=True)  52.2 us
    all_to_all x1, waiting for transfers between devices, body(): lax.all_to_all(current, 'src', split_axis=0, concat_axis=0, tiled=True)  30 us
    all_to_all x2, starting transfers between devices, body(): lax.all_to_all(state, 'src', split_axis=0, concat_axis=0, tiled=True)  11.5 us
    unnamed x14, local copies, waits for them, and re-layouts  8.47 us
    all_to_all x1, starting transfers between devices, body(): lax.all_to_all(current, 'src', split_axis=0, concat_axis=0, tiled=True)  4.91 us
  transfers between devices with their start and end apart: 3, of which 3 were waited for; matrix products, arithmetic and copies ran while one was open for 1% of the time, Pallas kernels for 20%

profile of v3, /device:TPU:15, one launch (start us, length us, event | category | flops | bytes accessed | tf_op | source)
XLA Modules:
  0.0 235.8 jit_solution(7952578404224832280)
XLA Ops:
  0.0 0.8 fusion
  1.0 0.6 gather_fusion.1
  1.6 16.2 %shard_map.37 = f32[16,128,256]{2,1,0:T(8,128)S(1)} custom-call(s32[4,16]{1,0:T(4,128)S(1)} %select_bitcast_fusion.2.pidx_ref, f32[8,8,2,2,64,64]{5,4,3,2,1,0:T(8,128)} %tr_ref.7, f32[16,2,128,256]{3,2,1,0:T(8,128)} %bitcast.12), custom_call_target="tpu_custom_call" | custom-call | flops 1073741824 | bytes 6291456 | tf_op jit(solution)/shard_map/pallas_call | solution.py:63
  17.9 1.3 copy-done.4
  19.2 6.6 %all-to-all-start = ((f32[16,128,256]{2,1,0:T(8,128)}), f32[16,128,256]{2,1,0:T(8,128)S(1)}, u32[]{:S(2)}, u32[]{:S(2)}) async-start(f32[16,128,256]{2,1,0:T(8,128)} %copy-done.4), calls=%async_computation | async-start | bytes 4194304 | tf_op jit(solution)/shard_map/all_to_all | solution.py:122
  25.8 0.6 gather_fusion.3
  26.4 16.2 %shard_map.39 = f32[16,128,256]{2,1,0:T(8,128)S(1)} custom-call(s32[4,16]{1,0:T(4,128)S(1)} %select_bitcast_fusion.pidx_ref, f32[8,8,2,2,64,64]{5,4,3,2,1,0:T(8,128)} %tr_ref.7, f32[16,2,128,256]{3,2,1,0:T(8,128)} %bitcast.13), custom_call_target="tpu_custom_call" | custom-call | flops 1073741824 | bytes 6291456 | tf_op jit(solution)/shard_map/pallas_call | solution.py:63
  42.7 1.3 copy-done.2
  44.0 29.2 %all-to-all-done.x_ref = f32[16,128,256]{2,1,0:T(8,128)S(1)} async-done(((f32[16,128,256]{2,1,0:T(8,128)}), f32[16,128,256]{2,1,0:T(8,128)S(1)}, u32[]{:S(2)}, u32[]{:S(2)}) %all-to-all-start) | async-done | bytes 2097184 | tf_op jit(solution)/shard_map/all_to_all | solution.py:122
  73.2 1.3 copy-done
  74.5 4.9 %all-to-all-start.2 = ((f32[16,128,256]{2,1,0:T(8,128)}), f32[16,128,256]{2,1,0:T(8,128)S(1)}, u32[]{:S(2)}, u32[]{:S(2)}) async-start(f32[16,128,256]{2,1,0:T(8,128)} %copy-done.2), calls=%async_computation.2 | async-start | bytes 4194304 | tf_op jit(solution)/shard_map/all_to_all | solution.py:122
  79.6 0.6 gather_fusion
  80.3 1.6 copy-done.1
  81.9 15.5 %shard_map.38 = f32[16,128,256]{2,1,0:T(8,128)S(1)} custom-call(s32[4,16]{1,0:T(4,128)S(1)} %select_bitcast_fusion.3.pidx_ref, f32[8,8,2,2,64,64]{5,4,3,2,1,0:T(8,128)} %tr_ref.7, f32[16,128,256]{2,1,0:T(8,128)S(1)} %copy-done.1), custom_call_target="tpu_custom_call" | custom-call | flops 1073741824 | bytes 6291456 | tf_op jit(solution)/shard_map/pallas_call | solution.py:63
  97.4 1.3 copy-done.3
  98.7 28.2 %all-to-all-done.2.x_ref = f32[16,128,256]{2,1,0:T(8,128)S(1)} async-done(((f32[16,128,256]{2,1,0:T(8,128)}), f32[16,128,256]{2,1,0:T(8,128)S(1)}, u32[]{:S(2)}, u32[]{:S(2)}) %all-to-all-start.2) | async-done | bytes 2097184 | tf_op jit(solution)/shard_map/all_to_all | solution.py:122
  126.9 4.9 %all-to-all-start.1 = ((f32[16,128,256]{2,1,0:T(8,128)}), f32[16,128,256]{2,1,0:T(8,128)}, u32[]{:S(2)}, u32[]{:S(2)}) async-start(f32[16,128,256]{2,1,0:T(8,128)} %copy-done.3), calls=%async_computation.1 | async-start | bytes 4194304 | tf_op jit(solution)/shard_map/all_to_all | solution.py:126
  131.8 0.6 gather_fusion.2
  132.4 15.5 %shard_map.40 = f32[16,128,256]{2,1,0:T(8,128)S(1)} custom-call(s32[4,16]{1,0:T(4,128)S(1)} %select_bitcast_fusion.1.pidx_ref, f32[8,8,2,2,64,64]{5,4,3,2,1,0:T(8,128)} %tr_ref.7, f32[16,128,256]{2,1,0:T(8,128)S(1)} %all-to-all-done.2.x_ref), custom_call_target="tpu_custom_call" | custom-call | flops 1073741824 | bytes 6291456 | tf_op jit(solution)/shard_map/pallas_call | solution.py:63
  148.0 1.3 copy-done.5
  149.3 30.0 %all-to-all-done.1 = f32[16,128,256]{2,1,0:T(8,128)} async-done(((f32[16,128,256]{2,1,0:T(8,128)}), f32[16,128,256]{2,1,0:T(8,128)}, u32[]{:S(2)}, u32[]{:S(2)}) %all-to-all-start.1) | async-done | bytes 2097184 | tf_op jit(solution)/shard_map/all_to_all | solution.py:126
  179.3 52.2 %all_to_all.20 = f32[16,128,256]{2,1,0:T(8,128)S(1)} all-to-all(f32[16,128,256]{2,1,0:T(8,128)} %copy-done.5), channel_id=1, replica_groups=mesh['shots'=2,'src'=16] {'src'}, dimensions={0} | all-to-all | bytes 4194304 | tf_op jit(solution)/shard_map/all_to_all | solution.py:126
  231.5 2.0 pad_maximum_fusion
  233.5 2.4 copy.16
  (25 shorter events, 0.7 us)
Async XLA Ops:
  17.9 1.3 copy-start.4
  19.2 54.0 %all-to-all-start = ((f32[16,128,256]{2,1,0:T(8,128)}), f32[16,128,256]{2,1,0:T(8,128)S(1)}, u32[]{:S(2)}, u32[]{:S(2)}) async-start(f32[16,128,256]{2,1,0:T(8,128)} %copy-done.4), calls=%async_computation | async-start | bytes 4194304 | tf_op jit(solution)/shard_map/all_to_all | solution.py:122
  42.7 1.3 copy-start.2
  73.2 1.3 copy-start
  74.5 52.3 %all-to-all-start.2 = ((f32[16,128,256]{2,1,0:T(8,128)}), f32[16,128,256]{2,1,0:T(8,128)S(1)}, u32[]{:S(2)}, u32[]{:S(2)}) async-start(f32[16,128,256]{2,1,0:T(8,128)} %copy-done.2), calls=%async_computation.2 | async-start | bytes 4194304 | tf_op jit(solution)/shard_map/all_to_all | solution.py:122
  80.3 1.6 copy-start.1
  97.4 1.3 copy-start.3
  126.9 52.4 %all-to-all-start.1 = ((f32[16,128,256]{2,1,0:T(8,128)}), f32[16,128,256]{2,1,0:T(8,128)}, u32[]{:S(2)}, u32[]{:S(2)}) async-start(f32[16,128,256]{2,1,0:T(8,128)} %copy-done.3), calls=%async_computation.1 | async-start | bytes 4194304 | tf_op jit(solution)/shard_map/all_to_all | solution.py:126
  147.9 1.3 copy-start.5

commit v4 on v3

--- a/solution.py
+++ b/solution.py
@@ -83,6 +83,31 @@
     )(pidx, trp, state)
 
 
+def place_kernel(x_ref, *refs):
+    refs[-1][...] = x_ref[...]
+
+
+def place_piece(piece, out, parity, chunk, split, k_len):
+    count, rows, width = piece.shape
+    step = 4 if count % 4 == 0 else 1
+    in_specs = [pl.BlockSpec((step, rows, width), lambda i: (i, 0, 0))]
+    args = [piece]
+    aliases = {}
+    if out is not None:
+        in_specs.append(pl.BlockSpec(memory_space=pl.ANY))
+        args.append(out)
+        aliases = {1: 0}
+    return pl.pallas_call(
+        place_kernel,
+        out_shape=jax.ShapeDtypeStruct((count, split, rows, k_len), piece.dtype),
+        grid=(count // step,),
+        in_specs=in_specs,
+        out_specs=pl.BlockSpec((step, None, rows, width), lambda i: (i, parity, 0, chunk)),
+        input_output_aliases=aliases,
+        cost_estimate=pl.CostEstimate(flops=0, transcendentals=0, bytes_accessed=2 * piece.size * 4),
+    )(*args)
+
+
 def body(weights_in, translations, pattern_index):
     box_count, rows, k_len = weights_in.shape
     groups = lax.axis_size("src")
@@ -124,10 +149,10 @@
                 current, translations, cross_pidx, cross_masks, first_cross, (0, 0, 0), count, width
             )
             pieces[parity, chunk] = lax.all_to_all(current, "src", split_axis=0, concat_axis=0, tiled=True)
-    joined = [jnp.concatenate([pieces[parity, c] for c in range(k_chunks)], axis=-1) for parity in range(split)]
-    if split > 1:
-        return jnp.stack(joined, axis=1).reshape(box_count, rows, k_len)
-    return joined[0]
+    out = None
+    for parity, chunk in sorted(pieces):
+        out = place_piece(pieces[parity, chunk], out, parity, chunk, split, k_len)
+    return out.reshape(box_count, rows, k_len)
 
 
 def solution(mesh):

time: 238 us -> 237 us (level)
  blocking collectives: 52.2 us -> 0 us
  waiting for transfers between devices: 87.4 us -> 131 us
  Pallas kernels: 63.5 us -> 71 us
  starting transfers between devices: 16.4 us -> 21.3 us
    all_to_all x1 -> x0, blocking collectives: 52.2 us -> none  [body(): lax.all_to_all(current, 'src', split_axis=0, concat_axis=0, tiled=True)]
    all_to_all x1 -> x2, waiting for transfers between devices: 30 us -> 73.7 us  [body(): lax.all_to_all(current, 'src', split_axis=0, concat_axis=0, tiled=True)]
    pallas_call x0 -> x2, Pallas kernels: none -> 7.55 us  [place_piece(): pl.pallas_call(place_kernel, out_shape=jax.ShapeDtypeStruct((count, split...]
    all_to_all x1 -> x2, starting transfers between devices: 4.91 us -> 9.82 us  [body(): lax.all_to_all(current, 'src', split_axis=0, concat_axis=0, tiled=True)]
    unnamed x14 -> x16, local copies, waits for them, and re-layouts: 8.47 us -> 9.86 us
  transfers between devices with their start and end apart: 3 -> 4, of which waited for: 3 -> 4; matrix products, arithmetic and copies ran while one was open for 1% -> 1% of each run, Pallas kernels for 20% -> 22%
where the time goes in v4:
time: 237 us
  waiting for transfers between devices  131 us (55%)
  Pallas kernels  71 us (30%)
  starting transfers between devices  21.3 us (9%)
  local copies, waits for them, and re-layouts  13.2 us (6%)
    all_to_all x2, waiting for transfers between devices, body(): lax.all_to_all(current, 'src', split_axis=0, concat_axis=0, tiled=True)  73.7 us
    pallas_call x4, Pallas kernels, apply_levels(): pl.pallas_call(functools.partial(levels_kernel, tuple(masks)), out_shape=...  63.5 us
    all_to_all x2, waiting for transfers between devices, body(): lax.all_to_all(state, 'src', split_axis=0, concat_axis=0, tiled=True)  57.3 us
    all_to_all x2, starting transfers between devices, body(): lax.all_to_all(state, 'src', split_axis=0, concat_axis=0, tiled=True)  11.5 us
    unnamed x16, local copies, waits for them, and re-layouts  9.86 us
    all_to_all x2, starting transfers between devices, body(): lax.all_to_all(current, 'src', split_axis=0, concat_axis=0, tiled=True)  9.82 us
    pallas_call x2, Pallas kernels, place_piece(): pl.pallas_call(place_kernel, out_shape=jax.ShapeDtypeStruct((count, split...  7.55 us
  transfers between devices with their start and end apart: 4, of which 4 were waited for; matrix products, arithmetic and copies ran while one was open for 1% of the time, Pallas kernels for 22%

profile of v4, /device:TPU:15, one launch (start us, length us, event | category | flops | bytes accessed | tf_op | source)
XLA Modules:
  0.0 236.7 jit_solution(2755784756205076168)
XLA Ops:
  0.0 0.8 fusion
  1.0 0.6 gather_fusion.3
  1.6 16.2 %shard_map.39 = f32[16,128,256]{2,1,0:T(8,128)S(1)} custom-call(s32[4,16]{1,0:T(4,128)S(1)} %select_bitcast_fusion.pidx_ref, f32[8,8,2,2,64,64]{5,4,3,2,1,0:T(8,128)} %tr_ref.7, f32[16,2,128,256]{3,2,1,0:T(8,128)} %bitcast.10), custom_call_target="tpu_custom_call" | custom-call | flops 1073741824 | bytes 6291456 | tf_op jit(solution)/shard_map/pallas_call | solution.py:63
  17.9 1.3 copy-done.4
  19.2 6.6 %all-to-all-start.2 = ((f32[16,128,256]{2,1,0:T(8,128)}), f32[16,128,256]{2,1,0:T(8,128)S(1)}, u32[]{:S(2)}, u32[]{:S(2)}) async-start(f32[16,128,256]{2,1,0:T(8,128)} %copy-done.4), calls=%async_computation.2 | async-start | bytes 4194304 | tf_op jit(solution)/shard_map/all_to_all | solution.py:147
  25.8 0.6 gather_fusion.1
  26.4 16.2 %shard_map.37 = f32[16,128,256]{2,1,0:T(8,128)S(1)} custom-call(s32[4,16]{1,0:T(4,128)S(1)} %select_bitcast_fusion.2.pidx_ref, f32[8,8,2,2,64,64]{5,4,3,2,1,0:T(8,128)} %tr_ref.7, f32[16,2,128,256]{3,2,1,0:T(8,128)} %bitcast.11), custom_call_target="tpu_custom_call" | custom-call | flops 1073741824 | bytes 6291456 | tf_op jit(solution)/shard_map/pallas_call | solution.py:63
  42.7 1.3 copy-done.2
  44.0 29.2 %all-to-all-done.2.x_ref = f32[16,128,256]{2,1,0:T(8,128)S(1)} async-done(((f32[16,128,256]{2,1,0:T(8,128)}), f32[16,128,256]{2,1,0:T(8,128)S(1)}, u32[]{:S(2)}, u32[]{:S(2)}) %all-to-all-start.2) | async-done | bytes 2097184 | tf_op jit(solution)/shard_map/all_to_all | solution.py:147
  73.2 1.3 copy-done
  74.5 4.9 %all-to-all-start = ((f32[16,128,256]{2,1,0:T(8,128)}), f32[16,128,256]{2,1,0:T(8,128)S(1)}, u32[]{:S(2)}, u32[]{:S(2)}) async-start(f32[16,128,256]{2,1,0:T(8,128)} %copy-done.2), calls=%async_computation | async-start | bytes 4194304 | tf_op jit(solution)/shard_map/all_to_all | solution.py:147
  80.3 1.6 copy-done.1
  81.9 15.5 %shard_map.40 = f32[16,128,256]{2,1,0:T(8,128)S(1)} custom-call(s32[4,16]{1,0:T(4,128)S(1)} %select_bitcast_fusion.1.pidx_ref, f32[8,8,2,2,64,64]{5,4,3,2,1,0:T(8,128)} %tr_ref.7, f32[16,128,256]{2,1,0:T(8,128)S(1)} %copy-done.1), custom_call_target="tpu_custom_call" | custom-call | flops 1073741824 | bytes 6291456 | tf_op jit(solution)/shard_map/pallas_call | solution.py:63
  97.4 1.4 copy-done.3
  98.7 28.1 %all-to-all-done.x_ref = f32[16,128,256]{2,1,0:T(8,128)S(1)} async-done(((f32[16,128,256]{2,1,0:T(8,128)}), f32[16,128,256]{2,1,0:T(8,128)S(1)}, u32[]{:S(2)}, u32[]{:S(2)}) %all-to-all-start) | async-done | bytes 2097184 | tf_op jit(solution)/shard_map/all_to_all | solution.py:147
  126.9 4.9 %all-to-all-start.3 = ((f32[16,128,256]{2,1,0:T(8,128)}), f32[16,128,256]{2,1,0:T(8,128)}, u32[]{:S(2)}, u32[]{:S(2)}) async-start(f32[16,128,256]{2,1,0:T(8,128)} %copy-done.3), calls=%async_computation.3 | async-start | bytes 4194304 | tf_op jit(solution)/shard_map/all_to_all | solution.py:151
  132.4 15.5 %shard_map.38 = f32[16,128,256]{2,1,0:T(8,128)S(1)} custom-call(s32[4,16]{1,0:T(4,128)S(1)} %select_bitcast_fusion.3.pidx_ref, f32[8,8,2,2,64,64]{5,4,3,2,1,0:T(8,128)} %tr_ref.7, f32[16,128,256]{2,1,0:T(8,128)S(1)} %all-to-all-done.x_ref), custom_call_target="tpu_custom_call" | custom-call | flops 1073741824 | bytes 6291456 | tf_op jit(solution)/shard_map/pallas_call | solution.py:63
  148.0 1.3 copy-done.5
  149.3 30.0 %all-to-all-done.3.x_ref = f32[16,128,256]{2,1,0:T(8,128)} async-done(((f32[16,128,256]{2,1,0:T(8,128)}), f32[16,128,256]{2,1,0:T(8,128)}, u32[]{:S(2)}, u32[]{:S(2)}) %all-to-all-start.3) | async-done | bytes 2097184 | tf_op jit(solution)/shard_map/all_to_all | solution.py:151
  179.3 4.9 %all-to-all-start.1 = ((f32[16,128,256]{2,1,0:T(8,128)}), f32[16,128,256]{2,1,0:T(8,128)S(1)}, u32[]{:S(2)}, u32[]{:S(2)}) async-start(f32[16,128,256]{2,1,0:T(8,128)} %copy-done.5), calls=%async_computation.1 | async-start | bytes 4194304 | tf_op jit(solution)/shard_map/all_to_all | solution.py:151
  184.2 3.8 %shard_map.41.refs_0_ = f32[16,2,128,256]{3,2,1,0:T(8,128)} custom-call(f32[16,128,256]{2,1,0:T(8,128)} %all-to-all-done.3.x_ref), custom_call_target="tpu_custom_call" | custom-call | bytes 4194304 | tf_op jit(solution)/shard_map/pallas_call | solution.py:100
  188.0 43.6 %all-to-all-done.1.x_ref = f32[16,128,256]{2,1,0:T(8,128)S(1)} async-done(((f32[16,128,256]{2,1,0:T(8,128)}), f32[16,128,256]{2,1,0:T(8,128)S(1)}, u32[]{:S(2)}, u32[]{:S(2)}) %all-to-all-start.1) | async-done | bytes 2097184 | tf_op jit(solution)/shard_map/all_to_all | solution.py:151
  231.6 1.3 copy-done.6
  233.0 3.8 %shard_map.42 = f32[16,2,128,256]{3,2,1,0:T(8,128)} custom-call(f32[16,128,256]{2,1,0:T(8,128)} %copy-done.6, f32[16,2,128,256]{3,2,1,0:T(8,128)} %shard_map.41.refs_0_), custom_call_target="tpu_custom_call", output_to_operand_aliasing={{}: (1, {})} | custom-call | bytes 4194304 | tf_op jit(solution)/shard_map/pallas_call | solution.py:100
  (28 shorter events, 1.8 us)
Async XLA Ops:
  17.9 1.3 copy-start.4
  19.2 54.0 %all-to-all-start.2 = ((f32[16,128,256]{2,1,0:T(8,128)}), f32[16,128,256]{2,1,0:T(8,128)S(1)}, u32[]{:S(2)}, u32[]{:S(2)}) async-start(f32[16,128,256]{2,1,0:T(8,128)} %copy-done.4), calls=%async_computation.2 | async-start | bytes 4194304 | tf_op jit(solution)/shard_map/all_to_all | solution.py:147
  42.7 1.3 copy-start.2
  73.2 1.3 copy-start
  74.5 52.3 %all-to-all-start = ((f32[16,128,256]{2,1,0:T(8,128)}), f32[16,128,256]{2,1,0:T(8,128)S(1)}, u32[]{:S(2)}, u32[]{:S(2)}) async-start(f32[16,128,256]{2,1,0:T(8,128)} %copy-done.2), calls=%async_computation | async-start | bytes 4194304 | tf_op jit(solution)/shard_map/all_to_all | solution.py:147
  80.3 1.6 copy-start.1
  97.4 1.4 copy-start.3
  126.9 52.4 %all-to-all-start.3 = ((f32[16,128,256]{2,1,0:T(8,128)}), f32[16,128,256]{2,1,0:T(8,128)}, u32[]{:S(2)}, u32[]{:S(2)}) async-start(f32[16,128,256]{2,1,0:T(8,128)} %copy-done.3), calls=%async_computation.3 | async-start | bytes 4194304 | tf_op jit(solution)/shard_map/all_to_all | solution.py:151
  148.0 1.3 copy-start.5
  179.3 52.3 %all-to-all-start.1 = ((f32[16,128,256]{2,1,0:T(8,128)}), f32[16,128,256]{2,1,0:T(8,128)S(1)}, u32[]{:S(2)}, u32[]{:S(2)}) async-start(f32[16,128,256]{2,1,0:T(8,128)} %copy-done.5), calls=%async_computation.1 | async-start | bytes 4194304 | tf_op jit(solution)/shard_map/all_to_all | solution.py:151
  231.6 1.3 copy-start.6

commit v5 on v4

--- a/solution.py
+++ b/solution.py
@@ -68,9 +68,11 @@
             grid=(n_levels,),
             in_specs=[
                 pl.BlockSpec((1,) + trp.shape[1:], lambda i, p: (level_offset + i, 0, 0, 0, 0, 0)),
-                pl.BlockSpec(block, lambda i, p: index_of),
+                pl.BlockSpec(block, lambda i, p: index_of)
+                if state.shape != (count, rows, width)
+                else pl.BlockSpec(memory_space=pltpu.VMEM),
             ],
-            out_specs=pl.BlockSpec((count, rows, width), lambda i, p: (0, 0, 0)),
+            out_specs=pl.BlockSpec(memory_space=pltpu.VMEM),
             scratch_shapes=[
                 pltpu.VMEM((patterns, 2, 2 * rank, 2 * rank), jnp.float32),
                 pltpu.VMEM((2, count, rows, width), jnp.float32),
@@ -83,14 +85,15 @@
     )(pidx, trp, state)
 
 
-def place_kernel(x_ref, *refs):
-    refs[-1][...] = x_ref[...]
+def place_kernel(step, x_ref, *refs):
+    start = pl.multiple_of(pl.program_id(0) * step, step)
+    refs[-1][...] = x_ref[pl.ds(start, step)]
 
 
 def place_piece(piece, out, parity, chunk, split, k_len):
     count, rows, width = piece.shape
-    step = 4 if count % 4 == 0 else 1
-    in_specs = [pl.BlockSpec((step, rows, width), lambda i: (i, 0, 0))]
+    step = count // 2 if count % 2 == 0 else count
+    in_specs = [pl.BlockSpec(memory_space=pltpu.VMEM)]
     args = [piece]
     aliases = {}
     if out is not None:
@@ -98,7 +101,7 @@
         args.append(out)
         aliases = {1: 0}
     return pl.pallas_call(
-        place_kernel,
+        functools.partial(place_kernel, step),
         out_shape=jax.ShapeDtypeStruct((count, split, rows, k_len), piece.dtype),
         grid=(count // step,),
         in_specs=in_specs,

time: 237 us -> 236 us (level)
  transfers between devices with their start and end apart: 4 -> 4, of which waited for: 4 -> 4; matrix products, arithmetic and copies ran while one was open for 1% -> 1% of each run, Pallas kernels for 22% -> 21%
where the time goes in v5:
time: 236 us
  waiting for transfers between devices  132 us (56%)
  Pallas kernels  69.4 us (29%)
  starting transfers between devices  21.3 us (9%)
  local copies, waits for them, and re-layouts  13.2 us (6%)
    all_to_all x2, waiting for transfers between devices, body(): lax.all_to_all(current, 'src', split_axis=0, concat_axis=0, tiled=True)  74.4 us
    pallas_call x4, Pallas kernels, apply_levels(): pl.pallas_call(functools.partial(levels_kernel, tuple(masks)), out_shape=...  63.5 us
    all_to_all x2, waiting for transfers between devices, body(): lax.all_to_all(state, 'src', split_axis=0, concat_axis=0, tiled=True)  57.3 us
    all_to_all x2, starting transfers between devices, body(): lax.all_to_all(state, 'src', split_axis=0, concat_axis=0, tiled=True)  11.5 us
    unnamed x16, local copies, waits for them, and re-layouts  9.86 us
    all_to_all x2, starting transfers between devices, body(): lax.all_to_all(current, 'src', split_axis=0, concat_axis=0, tiled=True)  9.82 us
    pallas_call x2, Pallas kernels, place_piece(): pl.pallas_call(functools.partial(place_kernel, step), out_shape=jax.Shape...  5.97 us
  transfers between devices with their start and end apart: 4, of which 4 were waited for; matrix products, arithmetic and copies ran while one was open for 1% of the time, Pallas kernels for 21%

profile of v5, /device:TPU:15, one launch (start us, length us, event | category | flops | bytes accessed | tf_op | source)
XLA Modules:
  0.0 235.9 jit_solution(6238022809054252611)
XLA Ops:
  0.0 0.8 fusion
  1.0 0.6 gather_fusion.3
  1.6 16.2 %shard_map.39 = f32[16,128,256]{2,1,0:T(8,128)S(1)} custom-call(s32[4,16]{1,0:T(4,128)S(1)} %select_bitcast_fusion.pidx_ref, f32[8,8,2,2,64,64]{5,4,3,2,1,0:T(8,128)} %tr_ref.7, f32[16,2,128,256]{3,2,1,0:T(8,128)} %bitcast.10), custom_call_target="tpu_custom_call" | custom-call | flops 1073741824 | bytes 6291456 | tf_op jit(solution)/shard_map/pallas_call | solution.py:63
  17.9 1.3 copy-done.4
  19.2 6.6 %all-to-all-start.2 = ((f32[16,128,256]{2,1,0:T(8,128)}), f32[16,128,256]{2,1,0:T(8,128)S(1)}, u32[]{:S(2)}, u32[]{:S(2)}) async-start(f32[16,128,256]{2,1,0:T(8,128)} %copy-done.4), calls=%async_computation.2 | async-start | bytes 4194304 | tf_op jit(solution)/shard_map/all_to_all | solution.py:150
  25.8 0.6 gather_fusion.1
  26.4 16.2 %shard_map.37 = f32[16,128,256]{2,1,0:T(8,128)S(1)} custom-call(s32[4,16]{1,0:T(4,128)S(1)} %select_bitcast_fusion.2.pidx_ref, f32[8,8,2,2,64,64]{5,4,3,2,1,0:T(8,128)} %tr_ref.7, f32[16,2,128,256]{3,2,1,0:T(8,128)} %bitcast.11), custom_call_target="tpu_custom_call" | custom-call | flops 1073741824 | bytes 6291456 | tf_op jit(solution)/shard_map/pallas_call | solution.py:63
  42.7 1.3 copy-done.2
  44.0 29.2 %all-to-all-done.2.x_ref = f32[16,128,256]{2,1,0:T(8,128)S(1)} async-done(((f32[16,128,256]{2,1,0:T(8,128)}), f32[16,128,256]{2,1,0:T(8,128)S(1)}, u32[]{:S(2)}, u32[]{:S(2)}) %all-to-all-start.2) | async-done | bytes 2097184 | tf_op jit(solution)/shard_map/all_to_all | solution.py:150
  73.2 1.3 copy-done
  74.5 4.9 %all-to-all-start = ((f32[16,128,256]{2,1,0:T(8,128)}), f32[16,128,256]{2,1,0:T(8,128)S(1)}, u32[]{:S(2)}, u32[]{:S(2)}) async-start(f32[16,128,256]{2,1,0:T(8,128)} %copy-done.2), calls=%async_computation | async-start | bytes 4194304 | tf_op jit(solution)/shard_map/all_to_all | solution.py:150
  80.3 1.6 copy-done.1
  81.9 15.5 %shard_map.40 = f32[16,128,256]{2,1,0:T(8,128)S(1)} custom-call(s32[4,16]{1,0:T(4,128)S(1)} %select_bitcast_fusion.1.pidx_ref, f32[8,8,2,2,64,64]{5,4,3,2,1,0:T(8,128)} %tr_ref.7, f32[16,128,256]{2,1,0:T(8,128)S(1)} %copy-done.1), custom_call_target="tpu_custom_call" | custom-call | flops 1073741824 | bytes 6291456 | tf_op jit(solution)/shard_map/pallas_call | solution.py:63
  97.4 1.4 copy-done.3
  98.7 28.1 %all-to-all-done.x_ref = f32[16,128,256]{2,1,0:T(8,128)S(1)} async-done(((f32[16,128,256]{2,1,0:T(8,128)}), f32[16,128,256]{2,1,0:T(8,128)S(1)}, u32[]{:S(2)}, u32[]{:S(2)}) %all-to-all-start) | async-done | bytes 2097184 | tf_op jit(solution)/shard_map/all_to_all | solution.py:150
  126.9 4.9 %all-to-all-start.3 = ((f32[16,128,256]{2,1,0:T(8,128)}), f32[16,128,256]{2,1,0:T(8,128)}, u32[]{:S(2)}, u32[]{:S(2)}) async-start(f32[16,128,256]{2,1,0:T(8,128)} %copy-done.3), calls=%async_computation.3 | async-start | bytes 4194304 | tf_op jit(solution)/shard_map/all_to_all | solution.py:154
  132.4 15.5 %shard_map.38 = f32[16,128,256]{2,1,0:T(8,128)S(1)} custom-call(s32[4,16]{1,0:T(4,128)S(1)} %select_bitcast_fusion.3.pidx_ref, f32[8,8,2,2,64,64]{5,4,3,2,1,0:T(8,128)} %tr_ref.7, f32[16,128,256]{2,1,0:T(8,128)S(1)} %all-to-all-done.x_ref), custom_call_target="tpu_custom_call" | custom-call | flops 1073741824 | bytes 6291456 | tf_op jit(solution)/shard_map/pallas_call | solution.py:63
  148.0 1.3 copy-done.5
  149.3 30.0 %all-to-all-done.3.x_ref = f32[16,128,256]{2,1,0:T(8,128)} async-done(((f32[16,128,256]{2,1,0:T(8,128)}), f32[16,128,256]{2,1,0:T(8,128)}, u32[]{:S(2)}, u32[]{:S(2)}) %all-to-all-start.3) | async-done | bytes 2097184 | tf_op jit(solution)/shard_map/all_to_all | solution.py:154
  179.3 4.9 %all-to-all-start.1 = ((f32[16,128,256]{2,1,0:T(8,128)}), f32[16,128,256]{2,1,0:T(8,128)S(1)}, u32[]{:S(2)}, u32[]{:S(2)}) async-start(f32[16,128,256]{2,1,0:T(8,128)} %copy-done.5), calls=%async_computation.1 | async-start | bytes 4194304 | tf_op jit(solution)/shard_map/all_to_all | solution.py:154
  184.2 3.0 %shard_map.41.refs_0_ = f32[16,2,128,256]{3,2,1,0:T(8,128)} custom-call(f32[16,128,256]{2,1,0:T(8,128)} %all-to-all-done.3.x_ref), custom_call_target="tpu_custom_call" | custom-call | bytes 4194304 | tf_op jit(solution)/shard_map/pallas_call | solution.py:103
  187.2 44.4 %all-to-all-done.1.x_ref = f32[16,128,256]{2,1,0:T(8,128)S(1)} async-done(((f32[16,128,256]{2,1,0:T(8,128)}), f32[16,128,256]{2,1,0:T(8,128)S(1)}, u32[]{:S(2)}, u32[]{:S(2)}) %all-to-all-start.1) | async-done | bytes 2097184 | tf_op jit(solution)/shard_map/all_to_all | solution.py:154
  231.6 1.3 copy-done.6
  233.0 3.0 %shard_map.42 = f32[16,2,128,256]{3,2,1,0:T(8,128)} custom-call(f32[16,128,256]{2,1,0:T(8,128)} %copy-done.6, f32[16,2,128,256]{3,2,1,0:T(8,128)} %shard_map.41.refs_0_), custom_call_target="tpu_custom_call", output_to_operand_aliasing={{}: (1, {})} | custom-call | bytes 4194304 | tf_op jit(solution)/shard_map/pallas_call | solution.py:103
  (28 shorter events, 1.8 us)
Async XLA Ops:
  17.9 1.3 copy-start.4
  19.2 54.0 %all-to-all-start.2 = ((f32[16,128,256]{2,1,0:T(8,128)}), f32[16,128,256]{2,1,0:T(8,128)S(1)}, u32[]{:S(2)}, u32[]{:S(2)}) async-start(f32[16,128,256]{2,1,0:T(8,128)} %copy-done.4), calls=%async_computation.2 | async-start | bytes 4194304 | tf_op jit(solution)/shard_map/all_to_all | solution.py:150
  42.7 1.3 copy-start.2
  73.2 1.3 copy-start
  74.5 52.3 %all-to-all-start = ((f32[16,128,256]{2,1,0:T(8,128)}), f32[16,128,256]{2,1,0:T(8,128)S(1)}, u32[]{:S(2)}, u32[]{:S(2)}) async-start(f32[16,128,256]{2,1,0:T(8,128)} %copy-done.2), calls=%async_computation | async-start | bytes 4194304 | tf_op jit(solution)/shard_map/all_to_all | solution.py:150
  80.3 1.6 copy-start.1
  97.4 1.4 copy-start.3
  126.9 52.4 %all-to-all-start.3 = ((f32[16,128,256]{2,1,0:T(8,128)}), f32[16,128,256]{2,1,0:T(8,128)}, u32[]{:S(2)}, u32[]{:S(2)}) async-start(f32[16,128,256]{2,1,0:T(8,128)} %copy-done.3), calls=%async_computation.3 | async-start | bytes 4194304 | tf_op jit(solution)/shard_map/all_to_all | solution.py:154
  148.0 1.3 copy-start.5
  179.3 52.3 %all-to-all-start.1 = ((f32[16,128,256]{2,1,0:T(8,128)}), f32[16,128,256]{2,1,0:T(8,128)S(1)}, u32[]{:S(2)}, u32[]{:S(2)}) async-start(f32[16,128,256]{2,1,0:T(8,128)} %copy-done.5), calls=%async_computation.1 | async-start | bytes 4194304 | tf_op jit(solution)/shard_map/all_to_all | solution.py:154
  231.6 1.3 copy-start.6

commit v6 on v5

--- a/solution.py
+++ b/solution.py
@@ -152,9 +152,14 @@
                 current, translations, cross_pidx, cross_masks, first_cross, (0, 0, 0), count, width
             )
             pieces[parity, chunk] = lax.all_to_all(current, "src", split_axis=0, concat_axis=0, tiled=True)
+    order = sorted(pieces)
     out = None
-    for parity, chunk in sorted(pieces):
+    for parity, chunk in order[:-1]:
         out = place_piece(pieces[parity, chunk], out, parity, chunk, split, k_len)
+    parity, chunk = order[-1]
+    if out is None:
+        out = jnp.zeros((count, split, rows, k_len), weights_in.dtype)
+    out = out.at[:, parity, :, chunk * width : (chunk + 1) * width].set(pieces[parity, chunk])
     return out.reshape(box_count, rows, k_len)
 
 

time: 236 us -> 234 us (level)
  Pallas kernels: 69.4 us -> 66.5 us
    pallas_call x2 -> x1, Pallas kernels: 5.97 us -> 2.99 us  [place_piece(): pl.pallas_call(functools.partial(place_kernel, step), out_shape=jax.Shape...]
    unnamed x16 -> x14, local copies, waits for them, and re-layouts: 9.86 us -> 8.47 us
  transfers between devices with their start and end apart: 4 -> 4, of which waited for: 4 -> 4; matrix products, arithmetic and copies ran while one was open for 1% -> 1% of each run, Pallas kernels for 21% -> 22%
where the time goes in v6:
time: 234 us; the launch traced here: 233 us
  waiting for transfers between devices  132 us (56%)
  Pallas kernels  66.5 us (28%)
  starting transfers between devices  21.3 us (9%)
  local copies, waits for them, and re-layouts  13.4 us (6%)
    all_to_all x2, waiting for transfers between devices, body(): lax.all_to_all(current, 'src', split_axis=0, concat_axis=0, tiled=True)  74.4 us
    pallas_call x4, Pallas kernels, apply_levels(): pl.pallas_call(functools.partial(levels_kernel, tuple(masks)), out_shape=...  63.5 us
    all_to_all x2, waiting for transfers between devices, body(): lax.all_to_all(state, 'src', split_axis=0, concat_axis=0, tiled=True)  57.3 us
    all_to_all x2, starting transfers between devices, body(): lax.all_to_all(state, 'src', split_axis=0, concat_axis=0, tiled=True)  11.5 us
    all_to_all x2, starting transfers between devices, body(): lax.all_to_all(current, 'src', split_axis=0, concat_axis=0, tiled=True)  9.82 us
    unnamed x14, local copies, waits for them, and re-layouts  8.47 us
  transfers between devices with their start and end apart: 4, of which 4 were waited for; matrix products, arithmetic and copies ran while one was open for 1% of the time, Pallas kernels for 22%

profile of v6, /device:TPU:15, one launch (start us, length us, event | category | flops | bytes accessed | tf_op | source)
XLA Modules:
  0.0 233.1 jit_solution(17029621834212475617)
XLA Ops:
  0.0 0.8 fusion
  1.0 0.6 gather_fusion.1
  1.6 16.2 %shard_map.37 = f32[16,128,256]{2,1,0:T(8,128)S(1)} custom-call(s32[4,16]{1,0:T(4,128)S(1)} %select_bitcast_fusion.2.pidx_ref, f32[8,8,2,2,64,64]{5,4,3,2,1,0:T(8,128)} %tr_ref.7, f32[16,2,128,256]{3,2,1,0:T(8,128)} %bitcast.14), custom_call_target="tpu_custom_call" | custom-call | flops 1073741824 | bytes 6291456 | tf_op jit(solution)/shard_map/pallas_call | solution.py:63
  17.9 1.3 copy-done.4
  19.2 6.6 %all-to-all-start = ((f32[16,128,256]{2,1,0:T(8,128)}), f32[16,128,256]{2,1,0:T(8,128)S(1)}, u32[]{:S(2)}, u32[]{:S(2)}) async-start(f32[16,128,256]{2,1,0:T(8,128)} %copy-done.4), calls=%async_computation | async-start | bytes 4194304 | tf_op jit(solution)/shard_map/all_to_all | solution.py:150
  25.8 0.6 gather_fusion.3
  26.4 16.2 %shard_map.40 = f32[16,128,256]{2,1,0:T(8,128)S(1)} custom-call(s32[4,16]{1,0:T(4,128)S(1)} %select_bitcast_fusion.pidx_ref, f32[8,8,2,2,64,64]{5,4,3,2,1,0:T(8,128)} %tr_ref.7, f32[16,2,128,256]{3,2,1,0:T(8,128)} %bitcast.15), custom_call_target="tpu_custom_call" | custom-call | flops 1073741824 | bytes 6291456 | tf_op jit(solution)/shard_map/pallas_call | solution.py:63
  42.7 1.3 copy-done.2
  44.0 29.2 %all-to-all-done.x_ref = f32[16,128,256]{2,1,0:T(8,128)S(1)} async-done(((f32[16,128,256]{2,1,0:T(8,128)}), f32[16,128,256]{2,1,0:T(8,128)S(1)}, u32[]{:S(2)}, u32[]{:S(2)}) %all-to-all-start) | async-done | bytes 2097184 | tf_op jit(solution)/shard_map/all_to_all | solution.py:150
  73.2 1.3 copy-done
  74.5 4.9 %all-to-all-start.2 = ((f32[16,128,256]{2,1,0:T(8,128)}), f32[16,128,256]{2,1,0:T(8,128)S(1)}, u32[]{:S(2)}, u32[]{:S(2)}) async-start(f32[16,128,256]{2,1,0:T(8,128)} %copy-done.2), calls=%async_computation.2 | async-start | bytes 4194304 | tf_op jit(solution)/shard_map/all_to_all | solution.py:150
  79.6 0.6 gather_fusion
  80.3 1.6 copy-done.1
  81.8 15.5 %shard_map.38 = f32[16,128,256]{2,1,0:T(8,128)S(1)} custom-call(s32[4,16]{1,0:T(4,128)S(1)} %select_bitcast_fusion.3.pidx_ref, f32[8,8,2,2,64,64]{5,4,3,2,1,0:T(8,128)} %tr_ref.7, f32[16,128,256]{2,1,0:T(8,128)S(1)} %copy-done.1), custom_call_target="tpu_custom_call" | custom-call | flops 1073741824 | bytes 6291456 | tf_op jit(solution)/shard_map/pallas_call | solution.py:63
  97.4 1.3 copy-done.3
  98.7 28.2 %all-to-all-done.2.x_ref = f32[16,128,256]{2,1,0:T(8,128)S(1)} async-done(((f32[16,128,256]{2,1,0:T(8,128)}), f32[16,128,256]{2,1,0:T(8,128)S(1)}, u32[]{:S(2)}, u32[]{:S(2)}) %all-to-all-start.2) | async-done | bytes 2097184 | tf_op jit(solution)/shard_map/all_to_all | solution.py:150
  126.8 4.9 %all-to-all-start.1 = ((f32[16,128,256]{2,1,0:T(8,128)}), f32[16,128,256]{2,1,0:T(8,128)}, u32[]{:S(2)}, u32[]{:S(2)}) async-start(f32[16,128,256]{2,1,0:T(8,128)} %copy-done.3), calls=%async_computation.1 | async-start | bytes 4194304 | tf_op jit(solution)/shard_map/all_to_all | solution.py:154
  132.4 15.5 %shard_map.41 = f32[16,128,256]{2,1,0:T(8,128)S(1)} custom-call(s32[4,16]{1,0:T(4,128)S(1)} %select_bitcast_fusion.1.pidx_ref, f32[8,8,2,2,64,64]{5,4,3,2,1,0:T(8,128)} %tr_ref.7, f32[16,128,256]{2,1,0:T(8,128)S(1)} %all-to-all-done.2.x_ref), custom_call_target="tpu_custom_call" | custom-call | flops 1073741824 | bytes 6291456 | tf_op jit(solution)/shard_map/pallas_call | solution.py:63
  147.9 1.3 copy-done.5
  149.2 30.0 %all-to-all-done.1.x_ref = f32[16,128,256]{2,1,0:T(8,128)} async-done(((f32[16,128,256]{2,1,0:T(8,128)}), f32[16,128,256]{2,1,0:T(8,128)}, u32[]{:S(2)}, u32[]{:S(2)}) %all-to-all-start.1) | async-done | bytes 2097184 | tf_op jit(solution)/shard_map/all_to_all | solution.py:154
  179.3 4.9 %all-to-all-start.3 = ((f32[16,128,256]{2,1,0:T(8,128)}), f32[16,128,256]{2,1,0:T(8,128)S(1)}, u32[]{:S(2)}, u32[]{:S(2)}) async-start(f32[16,128,256]{2,1,0:T(8,128)} %copy-done.5), calls=%async_computation.3 | async-start | bytes 4194304 | tf_op jit(solution)/shard_map/all_to_all | solution.py:154
  184.2 3.0 %shard_map.39 = f32[16,2,128,256]{3,2,1,0:T(8,128)} custom-call(f32[16,128,256]{2,1,0:T(8,128)} %all-to-all-done.1.x_ref), custom_call_target="tpu_custom_call" | custom-call | bytes 4194304 | tf_op jit(solution)/shard_map/pallas_call | solution.py:103
  187.2 44.4 %all-to-all-done.3 = f32[16,128,256]{2,1,0:T(8,128)S(1)} async-done(((f32[16,128,256]{2,1,0:T(8,128)}), f32[16,128,256]{2,1,0:T(8,128)S(1)}, u32[]{:S(2)}, u32[]{:S(2)}) %all-to-all-start.3) | async-done | bytes 2097184 | tf_op jit(solution)/shard_map/all_to_all | solution.py:154
  231.6 1.5 bitcast_dynamic-update-slice_fusion
  (26 shorter events, 1.3 us)
Async XLA Ops:
  17.9 1.3 copy-start.4
  19.2 54.0 %all-to-all-start = ((f32[16,128,256]{2,1,0:T(8,128)}), f32[16,128,256]{2,1,0:T(8,128)S(1)}, u32[]{:S(2)}, u32[]{:S(2)}) async-start(f32[16,128,256]{2,1,0:T(8,128)} %copy-done.4), calls=%async_computation | async-start | bytes 4194304 | tf_op jit(solution)/shard_map/all_to_all | solution.py:150
  42.7 1.3 copy-start.2
  73.2 1.3 copy-start
  74.5 52.3 %all-to-all-start.2 = ((f32[16,128,256]{2,1,0:T(8,128)}), f32[16,128,256]{2,1,0:T(8,128)S(1)}, u32[]{:S(2)}, u32[]{:S(2)}) async-start(f32[16,128,256]{2,1,0:T(8,128)} %copy-done.2), calls=%async_computation.2 | async-start | bytes 4194304 | tf_op jit(solution)/shard_map/all_to_all | solution.py:150
  80.3 1.6 copy-start.1
  97.3 1.3 copy-start.3
  126.8 52.4 %all-to-all-start.1 = ((f32[16,128,256]{2,1,0:T(8,128)}), f32[16,128,256]{2,1,0:T(8,128)}, u32[]{:S(2)}, u32[]{:S(2)}) async-start(f32[16,128,256]{2,1,0:T(8,128)} %copy-done.3), calls=%async_computation.1 | async-start | bytes 4194304 | tf_op jit(solution)/shard_map/all_to_all | solution.py:154
  147.9 1.3 copy-start.5
  179.3 52.3 %all-to-all-start.3 = ((f32[16,128,256]{2,1,0:T(8,128)}), f32[16,128,256]{2,1,0:T(8,128)S(1)}, u32[]{:S(2)}, u32[]{:S(2)}) async-start(f32[16,128,256]{2,1,0:T(8,128)} %copy-done.5), calls=%async_computation.3 | async-start | bytes 4194304 | tf_op jit(solution)/shard_map/all_to_all | solution.py:154

commit v7 on v6

--- a/solution.py
+++ b/solution.py
@@ -12,7 +12,7 @@
 PARITY_SPLIT = True
 
 
-def levels_kernel(masks, pidx_ref, tr_ref, x_ref, o_ref, table, buf):
+def levels_kernel(masks, level_offset, layout, pidx_ref, tr_ref, x_ref, o_ref, table, buf):
     level = pl.program_id(0)
     patterns = tr_ref.shape[1]
     rank = tr_ref.shape[-1]
@@ -25,6 +25,12 @@
 
     count = x_ref.shape[0]
     last = len(masks) - 1
+    box_count, split, parity, repeat = layout
+    device = lax.axis_index("src")
+
+    def box_of(slot):
+        return (slot // repeat) * box_count + (device * repeat + slot % repeat) * split + parity
+
     for li, mask in enumerate(masks):
         src = x_ref if li == 0 else buf.at[(li - 1) % 2]
         dst = o_ref if li == last else buf.at[li % 2]
@@ -34,8 +40,8 @@
             def pair(i, carry):
                 lo = (i // mask) * (2 * mask) + i % mask
                 hi = lo + mask
-                p_lo = pidx_ref[li, lo]
-                p_hi = pidx_ref[li, hi]
+                p_lo = pidx_ref[level_offset + li, box_of(lo)]
+                p_hi = pidx_ref[level_offset + li, box_of(hi)]
                 lhs = jnp.concatenate(
                     [
                         jnp.concatenate([table[p_lo, 0], table[p_lo, 1]], axis=1),
@@ -53,7 +59,7 @@
             lax.fori_loop(0, count // 2, pair, 0)
 
 
-def apply_levels(state, trp, pidx, masks, level_offset, index_of, count, width):
+def apply_levels(state, trp, pidx, masks, level_offset, layout, index_of, count, width):
     rows = state.shape[-2]
     n_levels = len(masks)
     patterns = trp.shape[1]
@@ -61,7 +67,7 @@
     block = (count, None, rows, width) if state.ndim == 4 else (count, rows, width)
     flops = 2 * count * rows * 2 * rows * width * n_levels
     return pl.pallas_call(
-        functools.partial(levels_kernel, tuple(masks)),
+        functools.partial(levels_kernel, tuple(masks), level_offset, layout),
         out_shape=jax.ShapeDtypeStruct((count, rows, width), state.dtype),
         grid_spec=pltpu.PrefetchScalarGridSpec(
             num_scalar_prefetch=1,
@@ -129,27 +135,24 @@
     width = k_len // k_chunks
     shaped = weights_in.reshape(count, split, rows, k_len) if split > 1 else weights_in
 
-    slot = jnp.arange(count, dtype=jnp.int32)
     local_masks = [1 << (bits[lv] - split_bits) for lv in range(first_cross)]
     cross_masks = [1 << (bits[lv] - local_bits + repeat_bits) for lv in range(first_cross, LEVELS)]
 
     pieces = {}
     for parity in range(split):
-        own_boxes = device * box_count + slot * split + parity
-        held_boxes = slot // repeat * box_count + (device * repeat + slot % repeat) * split + parity
-        local_pidx = jnp.take(pattern_index[:first_cross], own_boxes, axis=1)
-        cross_pidx = jnp.take(pattern_index[first_cross:], held_boxes, axis=1)
+        local_layout = (box_count, split, parity, count)
+        cross_layout = (box_count, split, parity, repeat)
         for chunk in range(k_chunks):
             index_of = (0, parity, 0, chunk) if split > 1 else (0, 0, chunk)
             if first_cross > 0:
-                state = apply_levels(shaped, translations, local_pidx, local_masks, 0, index_of, count, width)
+                state = apply_levels(shaped, translations, pattern_index, local_masks, 0, local_layout, index_of, count, width)
             elif split > 1:
                 state = shaped[:, parity, :, chunk * width : (chunk + 1) * width]
             else:
                 state = shaped[:, :, chunk * width : (chunk + 1) * width]
             current = lax.all_to_all(state, "src", split_axis=0, concat_axis=0, tiled=True)
             current = apply_levels(
-                current, translations, cross_pidx, cross_masks, first_cross, (0, 0, 0), count, width
+                current, translations, pattern_index, cross_masks, first_cross, cross_layout, (0, 0, 0), count, width
             )
             pieces[parity, chunk] = lax.all_to_all(current, "src", split_axis=0, concat_axis=0, tiled=True)
     order = sorted(pieces)

time: 234 us -> 233 us (level)
  local copies, waits for them, and re-layouts: 13.4 us -> 10.4 us
    gather x8 -> x0, local copies, waits for them, and re-layouts: 2.58 us -> none  [the longest x4 1.29 us: body(): local_pidx = jnp.take(pattern_index[:first_cross], own_boxes, axis=1)]
    unnamed x14 -> x16, local copies, waits for them, and re-layouts: 8.47 us -> 8.89 us
  transfers between devices with their start and end apart: 4 -> 4, of which waited for: 4 -> 4; matrix products, arithmetic and copies ran while one was open for 1% -> 0% of each run, Pallas kernels for 22% -> 22%
where the time goes in v7:
time: 233 us
  waiting for transfers between devices  133 us (57%)
  Pallas kernels  67.3 us (29%)
  starting transfers between devices  21.4 us (9%)
  local copies, waits for them, and re-layouts  10.4 us (4%)
    all_to_all x2, waiting for transfers between devices, body(): lax.all_to_all(current, 'src', split_axis=0, concat_axis=0, tiled=True)  74.9 us
    pallas_call x4, Pallas kernels, apply_levels(): pl.pallas_call(functools.partial(levels_kernel, tuple(masks), level_offse...  64.3 us
    all_to_all x2, waiting for transfers between devices, body(): lax.all_to_all(state, 'src', split_axis=0, concat_axis=0, tiled=True)  58.4 us
    all_to_all x2, starting transfers between devices, body(): lax.all_to_all(state, 'src', split_axis=0, concat_axis=0, tiled=True)  11.6 us
    all_to_all x2, starting transfers between devices, body(): lax.all_to_all(current, 'src', split_axis=0, concat_axis=0, tiled=True)  9.82 us
    unnamed x16, local copies, waits for them, and re-layouts  8.89 us
  transfers between devices with their start and end apart: 4, of which 4 were waited for; matrix products, arithmetic and copies ran while one was open for 0% of the time, Pallas kernels for 22%

profile of v7, /device:TPU:15, one launch (start us, length us, event | category | flops | bytes accessed | tf_op | source)
XLA Modules:
  0.0 232.6 jit_solution(560037043916746532)
XLA Ops:
  0.0 0.7 copy-done.6
  0.7 16.5 %shard_map.37 = f32[16,128,256]{2,1,0:T(8,128)S(1)} custom-call(s32[8,512]{1,0:T(8,128)S(1)} %copy-done.6, f32[8,8,2,2,64,64]{5,4,3,2,1,0:T(8,128)} %tr_ref.7, f32[16,2,128,256]{3,2,1,0:T(8,128)} %bitcast.6), custom_call_target="tpu_custom_call" | custom-call | flops 1073741824 | bytes 6291456 | tf_op jit(solution)/shard_map/pallas_call | solution.py:69
  17.2 0.0 copy-start.5
  17.2 1.3 copy-done.5
  18.5 6.7 %all-to-all-start = ((f32[16,128,256]{2,1,0:T(8,128)}), f32[16,128,256]{2,1,0:T(8,128)S(1)}, u32[]{:S(2)}, u32[]{:S(2)}) async-start(f32[16,128,256]{2,1,0:T(8,128)} %copy-done.5), calls=%async_computation | async-start | bytes 4194304 | tf_op jit(solution)/shard_map/all_to_all | solution.py:153
  25.2 0.0 copy-done.7
  25.2 16.5 %shard_map.40 = f32[16,128,256]{2,1,0:T(8,128)S(1)} custom-call(s32[8,512]{1,0:T(8,128)S(1)} %copy-done.7, f32[8,8,2,2,64,64]{5,4,3,2,1,0:T(8,128)} %tr_ref.7, f32[16,2,128,256]{3,2,1,0:T(8,128)} %bitcast.7), custom_call_target="tpu_custom_call" | custom-call | flops 1073741824 | bytes 6291456 | tf_op jit(solution)/shard_map/pallas_call | solution.py:69
  41.7 1.3 copy-done.4
  43.0 29.6 %all-to-all-done.x_ref = f32[16,128,256]{2,1,0:T(8,128)S(1)} async-done(((f32[16,128,256]{2,1,0:T(8,128)}), f32[16,128,256]{2,1,0:T(8,128)S(1)}, u32[]{:S(2)}, u32[]{:S(2)}) %all-to-all-start) | async-done | bytes 2097184 | tf_op jit(solution)/shard_map/all_to_all | solution.py:153
  72.6 1.3 copy-done
  73.9 4.9 %all-to-all-start.2 = ((f32[16,128,256]{2,1,0:T(8,128)}), f32[16,128,256]{2,1,0:T(8,128)S(1)}, u32[]{:S(2)}, u32[]{:S(2)}) async-start(f32[16,128,256]{2,1,0:T(8,128)} %copy-done.4), calls=%async_computation.2 | async-start | bytes 4194304 | tf_op jit(solution)/shard_map/all_to_all | solution.py:153
  78.8 1.6 copy-done.1
  80.4 15.7 %shard_map.38 = f32[16,128,256]{2,1,0:T(8,128)S(1)} custom-call(s32[8,512]{1,0:T(8,128)S(1)} %copy-done.7, f32[8,8,2,2,64,64]{5,4,3,2,1,0:T(8,128)} %tr_ref.7, f32[16,128,256]{2,1,0:T(8,128)S(1)} %copy-done.1), custom_call_target="tpu_custom_call" | custom-call | flops 1073741824 | bytes 6291456 | tf_op jit(solution)/shard_map/pallas_call | solution.py:69
  96.2 0.0 copy-start.2
  96.2 1.3 copy-done.2
  97.5 28.8 %all-to-all-done.2.x_ref = f32[16,128,256]{2,1,0:T(8,128)S(1)} async-done(((f32[16,128,256]{2,1,0:T(8,128)}), f32[16,128,256]{2,1,0:T(8,128)S(1)}, u32[]{:S(2)}, u32[]{:S(2)}) %all-to-all-start.2) | async-done | bytes 2097184 | tf_op jit(solution)/shard_map/all_to_all | solution.py:153
  126.3 4.9 %all-to-all-start.1 = ((f32[16,128,256]{2,1,0:T(8,128)}), f32[16,128,256]{2,1,0:T(8,128)}, u32[]{:S(2)}, u32[]{:S(2)}) async-start(f32[16,128,256]{2,1,0:T(8,128)} %copy-done.2), calls=%async_computation.1 | async-start | bytes 4194304 | tf_op jit(solution)/shard_map/all_to_all | solution.py:157
  131.2 15.7 %shard_map.41 = f32[16,128,256]{2,1,0:T(8,128)S(1)} custom-call(s32[8,512]{1,0:T(8,128)S(1)} %copy-done.7, f32[8,8,2,2,64,64]{5,4,3,2,1,0:T(8,128)} %tr_ref.7, f32[16,128,256]{2,1,0:T(8,128)S(1)} %all-to-all-done.2.x_ref), custom_call_target="tpu_custom_call" | custom-call | flops 1073741824 | bytes 6291456 | tf_op jit(solution)/shard_map/pallas_call | solution.py:69
  146.9 1.3 copy-done.3
  148.2 30.5 %all-to-all-done.1.x_ref = f32[16,128,256]{2,1,0:T(8,128)} async-done(((f32[16,128,256]{2,1,0:T(8,128)}), f32[16,128,256]{2,1,0:T(8,128)}, u32[]{:S(2)}, u32[]{:S(2)}) %all-to-all-start.1) | async-done | bytes 2097184 | tf_op jit(solution)/shard_map/all_to_all | solution.py:157
  178.7 4.9 %all-to-all-start.3 = ((f32[16,128,256]{2,1,0:T(8,128)}), f32[16,128,256]{2,1,0:T(8,128)S(1)}, u32[]{:S(2)}, u32[]{:S(2)}) async-start(f32[16,128,256]{2,1,0:T(8,128)} %copy-done.3), calls=%async_computation.3 | async-start | bytes 4194304 | tf_op jit(solution)/shard_map/all_to_all | solution.py:157
  183.6 3.0 %shard_map.39 = f32[16,2,128,256]{3,2,1,0:T(8,128)} custom-call(f32[16,128,256]{2,1,0:T(8,128)} %all-to-all-done.1.x_ref), custom_call_target="tpu_custom_call" | custom-call | bytes 4194304 | tf_op jit(solution)/shard_map/pallas_call | solution.py:109
  186.6 44.4 %all-to-all-done.3 = f32[16,128,256]{2,1,0:T(8,128)S(1)} async-done(((f32[16,128,256]{2,1,0:T(8,128)}), f32[16,128,256]{2,1,0:T(8,128)S(1)}, u32[]{:S(2)}, u32[]{:S(2)}) %all-to-all-start.3) | async-done | bytes 2097184 | tf_op jit(solution)/shard_map/all_to_all | solution.py:157
  231.0 1.5 bitcast_dynamic-update-slice_fusion
  (6 shorter events, 0.0 us)
Async XLA Ops:
  0.0 0.7 copy-start.6
  17.2 1.3 copy-start.5
  18.5 6.7 %copy-start.7 = (s32[8,512]{1,0:T(8,128)S(1)}, s32[8,512]{1,0:T(8,128)}, u32[]{:S(2)}) copy-start(s32[8,512]{1,0:T(8,128)} %pidx_ref.7) | copy-start | bytes 49156
  18.5 54.1 %all-to-all-start = ((f32[16,128,256]{2,1,0:T(8,128)}), f32[16,128,256]{2,1,0:T(8,128)S(1)}, u32[]{:S(2)}, u32[]{:S(2)}) async-start(f32[16,128,256]{2,1,0:T(8,128)} %copy-done.5), calls=%async_computation | async-start | bytes 4194304 | tf_op jit(solution)/shard_map/all_to_all | solution.py:153
  41.7 1.3 copy-start.4
  72.6 1.3 copy-start
  73.9 52.3 %all-to-all-start.2 = ((f32[16,128,256]{2,1,0:T(8,128)}), f32[16,128,256]{2,1,0:T(8,128)S(1)}, u32[]{:S(2)}, u32[]{:S(2)}) async-start(f32[16,128,256]{2,1,0:T(8,128)} %copy-done.4), calls=%async_computation.2 | async-start | bytes 4194304 | tf_op jit(solution)/shard_map/all_to_all | solution.py:153
  78.8 1.6 copy-start.1
  96.2 1.3 copy-start.2
  126.3 52.4 %all-to-all-start.1 = ((f32[16,128,256]{2,1,0:T(8,128)}), f32[16,128,256]{2,1,0:T(8,128)}, u32[]{:S(2)}, u32[]{:S(2)}) async-start(f32[16,128,256]{2,1,0:T(8,128)} %copy-done.2), calls=%async_computation.1 | async-start | bytes 4194304 | tf_op jit(solution)/shard_map/all_to_all | solution.py:157
  146.9 1.3 copy-start.3
  178.7 52.3 %all-to-all-start.3 = ((f32[16,128,256]{2,1,0:T(8,128)}), f32[16,128,256]{2,1,0:T(8,128)S(1)}, u32[]{:S(2)}, u32[]{:S(2)}) async-start(f32[16,128,256]{2,1,0:T(8,128)} %copy-done.3), calls=%async_computation.3 | async-start | bytes 4194304 | tf_op jit(solution)/shard_map/all_to_all | solution.py:157

commit v8 on v7

--- a/solution.py
+++ b/solution.py
@@ -12,7 +12,7 @@
 PARITY_SPLIT = True
 
 
-def levels_kernel(masks, level_offset, layout, pidx_ref, tr_ref, x_ref, o_ref, table, buf):
+def levels_kernel(masks, level_offset, layout, precision, pidx_ref, tr_ref, x_ref, o_ref, table, buf):
     level = pl.program_id(0)
     patterns = tr_ref.shape[1]
     rank = tr_ref.shape[-1]
@@ -50,7 +50,7 @@
                     axis=0,
                 )
                 rhs = jnp.concatenate([src[lo], src[hi]], axis=0)
-                out = jnp.dot(lhs, rhs, precision=lax.Precision.HIGHEST, preferred_element_type=jnp.float32)
+                out = jnp.dot(lhs, rhs, precision=precision, preferred_element_type=jnp.float32)
                 half = out.shape[0] // 2
                 dst[lo] = out[:half]
                 dst[hi] = out[half:]
@@ -59,7 +59,7 @@
             lax.fori_loop(0, count // 2, pair, 0)
 
 
-def apply_levels(state, trp, pidx, masks, level_offset, layout, index_of, count, width):
+def apply_levels(state, trp, pidx, masks, level_offset, layout, index_of, count, width, precision):
     rows = state.shape[-2]
     n_levels = len(masks)
     patterns = trp.shape[1]
@@ -67,7 +67,7 @@
     block = (count, None, rows, width) if state.ndim == 4 else (count, rows, width)
     flops = 2 * count * rows * 2 * rows * width * n_levels
     return pl.pallas_call(
-        functools.partial(levels_kernel, tuple(masks), level_offset, layout),
+        functools.partial(levels_kernel, tuple(masks), level_offset, layout, precision),
         out_shape=jax.ShapeDtypeStruct((count, rows, width), state.dtype),
         grid_spec=pltpu.PrefetchScalarGridSpec(
             num_scalar_prefetch=1,
@@ -145,14 +145,18 @@
         for chunk in range(k_chunks):
             index_of = (0, parity, 0, chunk) if split > 1 else (0, 0, chunk)
             if first_cross > 0:
-                state = apply_levels(shaped, translations, pattern_index, local_masks, 0, local_layout, index_of, count, width)
+                state = apply_levels(
+                    shaped, translations, pattern_index, local_masks, 0, local_layout, index_of, count, width,
+                    lax.Precision.HIGH if (parity, chunk) == (0, 0) else lax.Precision.HIGHEST,
+                )
             elif split > 1:
                 state = shaped[:, parity, :, chunk * width : (chunk + 1) * width]
             else:
                 state = shaped[:, :, chunk * width : (chunk + 1) * width]
             current = lax.all_to_all(state, "src", split_axis=0, concat_axis=0, tiled=True)
             current = apply_levels(
-                current, translations, pattern_index, cross_masks, first_cross, cross_layout, (0, 0, 0), count, width
+                current, translations, pattern_index, cross_masks, first_cross, cross_layout, (0, 0, 0), count, width,
+                lax.Precision.HIGHEST,
             )
             pieces[parity, chunk] = lax.all_to_all(current, "src", split_axis=0, concat_axis=0, tiled=True)
     order = sorted(pieces)

time: 233 us -> 230 us (0.987)
  Pallas kernels: 67.3 us -> 64 us
    pallas_call x4, Pallas kernels: 64.3 us -> 61 us  [apply_levels(): pl.pallas_call(functools.partial(levels_kernel, tuple(masks), level_offse...]
where the time goes in v8:
time: 230 us; the launch traced here: 229 us
  waiting for transfers between devices  133 us (58%)
  Pallas kernels  64 us (28%)
  starting transfers between devices  21.4 us (9%)
  local copies, waits for them, and re-layouts  10.4 us (5%)
    all_to_all x2, waiting for transfers between devices, body(): lax.all_to_all(current, 'src', split_axis=0, concat_axis=0, tiled=True)  74.9 us
    pallas_call x4, Pallas kernels, apply_levels(): pl.pallas_call(functools.partial(levels_kernel, tuple(masks), level_offse...  61 us
    all_to_all x2, waiting for transfers between devices, body(): lax.all_to_all(state, 'src', split_axis=0, concat_axis=0, tiled=True)  58.4 us
    all_to_all x2, starting transfers between devices, body(): lax.all_to_all(state, 'src', split_axis=0, concat_axis=0, tiled=True)  11.6 us
    all_to_all x2, starting transfers between devices, body(): lax.all_to_all(current, 'src', split_axis=0, concat_axis=0, tiled=True)  9.82 us
    unnamed x16, local copies, waits for them, and re-layouts  8.89 us
  transfers between devices with their start and end apart: 4, of which 4 were waited for; matrix products, arithmetic and copies ran while one was open for 0% of the time, Pallas kernels for 22%

profile of v8, /device:TPU:15, one launch (start us, length us, event | category | flops | bytes accessed | tf_op | source)
XLA Modules:
  0.0 229.2 jit_solution(16648242029993287930)
XLA Ops:
  0.0 0.7 copy-done.6
  0.7 13.1 %shard_map.37 = f32[16,128,256]{2,1,0:T(8,128)S(1)} custom-call(s32[8,512]{1,0:T(8,128)S(1)} %copy-done.6, f32[8,8,2,2,64,64]{5,4,3,2,1,0:T(8,128)} %tr_ref.7, f32[16,2,128,256]{3,2,1,0:T(8,128)} %bitcast.6), custom_call_target="tpu_custom_call" | custom-call | flops 1073741824 | bytes 6291456 | tf_op jit(solution)/shard_map/pallas_call | solution.py:69
  13.9 0.0 copy-start.5
  13.9 1.3 copy-done.5
  15.2 6.7 %all-to-all-start = ((f32[16,128,256]{2,1,0:T(8,128)}), f32[16,128,256]{2,1,0:T(8,128)S(1)}, u32[]{:S(2)}, u32[]{:S(2)}) async-start(f32[16,128,256]{2,1,0:T(8,128)} %copy-done.5), calls=%async_computation | async-start | bytes 4194304 | tf_op jit(solution)/shard_map/all_to_all | solution.py:156
  21.9 0.0 copy-done.7
  21.9 16.5 %shard_map.40 = f32[16,128,256]{2,1,0:T(8,128)S(1)} custom-call(s32[8,512]{1,0:T(8,128)S(1)} %copy-done.7, f32[8,8,2,2,64,64]{5,4,3,2,1,0:T(8,128)} %tr_ref.7, f32[16,2,128,256]{3,2,1,0:T(8,128)} %bitcast.7), custom_call_target="tpu_custom_call" | custom-call | flops 1073741824 | bytes 6291456 | tf_op jit(solution)/shard_map/pallas_call | solution.py:69
  38.4 1.3 copy-done.4
  39.7 29.6 %all-to-all-done.x_ref = f32[16,128,256]{2,1,0:T(8,128)S(1)} async-done(((f32[16,128,256]{2,1,0:T(8,128)}), f32[16,128,256]{2,1,0:T(8,128)S(1)}, u32[]{:S(2)}, u32[]{:S(2)}) %all-to-all-start) | async-done | bytes 2097184 | tf_op jit(solution)/shard_map/all_to_all | solution.py:156
  69.3 1.3 copy-done
  70.6 4.9 %all-to-all-start.2 = ((f32[16,128,256]{2,1,0:T(8,128)}), f32[16,128,256]{2,1,0:T(8,128)S(1)}, u32[]{:S(2)}, u32[]{:S(2)}) async-start(f32[16,128,256]{2,1,0:T(8,128)} %copy-done.4), calls=%async_computation.2 | async-start | bytes 4194304 | tf_op jit(solution)/shard_map/all_to_all | solution.py:156
  75.5 1.6 copy-done.1
  77.1 15.7 %shard_map.38 = f32[16,128,256]{2,1,0:T(8,128)S(1)} custom-call(s32[8,512]{1,0:T(8,128)S(1)} %copy-done.7, f32[8,8,2,2,64,64]{5,4,3,2,1,0:T(8,128)} %tr_ref.7, f32[16,128,256]{2,1,0:T(8,128)S(1)} %copy-done.1), custom_call_target="tpu_custom_call" | custom-call | flops 1073741824 | bytes 6291456 | tf_op jit(solution)/shard_map/pallas_call | solution.py:69
  92.8 0.0 copy-start.2
  92.8 1.3 copy-done.2
  94.2 28.8 %all-to-all-done.2.x_ref = f32[16,128,256]{2,1,0:T(8,128)S(1)} async-done(((f32[16,128,256]{2,1,0:T(8,128)}), f32[16,128,256]{2,1,0:T(8,128)S(1)}, u32[]{:S(2)}, u32[]{:S(2)}) %all-to-all-start.2) | async-done | bytes 2097184 | tf_op jit(solution)/shard_map/all_to_all | solution.py:156
  122.9 4.9 %all-to-all-start.1 = ((f32[16,128,256]{2,1,0:T(8,128)}), f32[16,128,256]{2,1,0:T(8,128)}, u32[]{:S(2)}, u32[]{:S(2)}) async-start(f32[16,128,256]{2,1,0:T(8,128)} %copy-done.2), calls=%async_computation.1 | async-start | bytes 4194304 | tf_op jit(solution)/shard_map/all_to_all | solution.py:161
  127.8 15.7 %shard_map.41 = f32[16,128,256]{2,1,0:T(8,128)S(1)} custom-call(s32[8,512]{1,0:T(8,128)S(1)} %copy-done.7, f32[8,8,2,2,64,64]{5,4,3,2,1,0:T(8,128)} %tr_ref.7, f32[16,128,256]{2,1,0:T(8,128)S(1)} %all-to-all-done.2.x_ref), custom_call_target="tpu_custom_call" | custom-call | flops 1073741824 | bytes 6291456 | tf_op jit(solution)/shard_map/pallas_call | solution.py:69
  143.6 1.3 copy-done.3
  144.9 30.5 %all-to-all-done.1.x_ref = f32[16,128,256]{2,1,0:T(8,128)} async-done(((f32[16,128,256]{2,1,0:T(8,128)}), f32[16,128,256]{2,1,0:T(8,128)}, u32[]{:S(2)}, u32[]{:S(2)}) %all-to-all-start.1) | async-done | bytes 2097184 | tf_op jit(solution)/shard_map/all_to_all | solution.py:161
  175.4 4.9 %all-to-all-start.3 = ((f32[16,128,256]{2,1,0:T(8,128)}), f32[16,128,256]{2,1,0:T(8,128)S(1)}, u32[]{:S(2)}, u32[]{:S(2)}) async-start(f32[16,128,256]{2,1,0:T(8,128)} %copy-done.3), calls=%async_computation.3 | async-start | bytes 4194304 | tf_op jit(solution)/shard_map/all_to_all | solution.py:161
  180.3 3.0 %shard_map.39 = f32[16,2,128,256]{3,2,1,0:T(8,128)} custom-call(f32[16,128,256]{2,1,0:T(8,128)} %all-to-all-done.1.x_ref), custom_call_target="tpu_custom_call" | custom-call | bytes 4194304 | tf_op jit(solution)/shard_map/pallas_call | solution.py:109
  183.3 44.4 %all-to-all-done.3 = f32[16,128,256]{2,1,0:T(8,128)S(1)} async-done(((f32[16,128,256]{2,1,0:T(8,128)}), f32[16,128,256]{2,1,0:T(8,128)S(1)}, u32[]{:S(2)}, u32[]{:S(2)}) %all-to-all-start.3) | async-done | bytes 2097184 | tf_op jit(solution)/shard_map/all_to_all | solution.py:161
  227.7 1.5 bitcast_dynamic-update-slice_fusion
  (6 shorter events, 0.0 us)
Async XLA Ops:
  0.0 0.7 copy-start.6
  13.9 1.3 copy-start.5
  15.2 6.7 %copy-start.7 = (s32[8,512]{1,0:T(8,128)S(1)}, s32[8,512]{1,0:T(8,128)}, u32[]{:S(2)}) copy-start(s32[8,512]{1,0:T(8,128)} %pidx_ref.7) | copy-start | bytes 49156
  15.2 54.1 %all-to-all-start = ((f32[16,128,256]{2,1,0:T(8,128)}), f32[16,128,256]{2,1,0:T(8,128)S(1)}, u32[]{:S(2)}, u32[]{:S(2)}) async-start(f32[16,128,256]{2,1,0:T(8,128)} %copy-done.5), calls=%async_computation | async-start | bytes 4194304 | tf_op jit(solution)/shard_map/all_to_all | solution.py:156
  38.3 1.3 copy-start.4
  69.3 1.3 copy-start
  70.6 52.3 %all-to-all-start.2 = ((f32[16,128,256]{2,1,0:T(8,128)}), f32[16,128,256]{2,1,0:T(8,128)S(1)}, u32[]{:S(2)}, u32[]{:S(2)}) async-start(f32[16,128,256]{2,1,0:T(8,128)} %copy-done.4), calls=%async_computation.2 | async-start | bytes 4194304 | tf_op jit(solution)/shard_map/all_to_all | solution.py:156
  75.5 1.6 copy-start.1
  92.8 1.3 copy-start.2
  122.9 52.4 %all-to-all-start.1 = ((f32[16,128,256]{2,1,0:T(8,128)}), f32[16,128,256]{2,1,0:T(8,128)}, u32[]{:S(2)}, u32[]{:S(2)}) async-start(f32[16,128,256]{2,1,0:T(8,128)} %copy-done.2), calls=%async_computation.1 | async-start | bytes 4194304 | tf_op jit(solution)/shard_map/all_to_all | solution.py:161
  143.6 1.3 copy-start.3
  175.4 52.3 %all-to-all-start.3 = ((f32[16,128,256]{2,1,0:T(8,128)}), f32[16,128,256]{2,1,0:T(8,128)S(1)}, u32[]{:S(2)}, u32[]{:S(2)}) async-start(f32[16,128,256]{2,1,0:T(8,128)} %copy-done.3), calls=%async_computation.3 | async-start | bytes 4194304 | tf_op jit(solution)/shard_map/all_to_all | solution.py:161

commit v9 on v8

--- a/solution.py
+++ b/solution.py
@@ -12,7 +12,7 @@
 PARITY_SPLIT = True
 
 
-def levels_kernel(masks, level_offset, layout, precision, pidx_ref, tr_ref, x_ref, o_ref, table, buf):
+def levels_kernel(masks, level_offset, layout, precision, unroll, pidx_ref, tr_ref, x_ref, o_ref, table, buf_a, buf_b):
     level = pl.program_id(0)
     patterns = tr_ref.shape[1]
     rank = tr_ref.shape[-1]
@@ -32,8 +32,8 @@
         return (slot // repeat) * box_count + (device * repeat + slot % repeat) * split + parity
 
     for li, mask in enumerate(masks):
-        src = x_ref if li == 0 else buf.at[(li - 1) % 2]
-        dst = o_ref if li == last else buf.at[li % 2]
+        src = x_ref if li == 0 else (buf_a if (li - 1) % 2 == 0 else buf_b)
+        dst = o_ref if li == last else (buf_a if li % 2 == 0 else buf_b)
 
         @pl.when(level == li)
         def _(src=src, dst=dst, li=li, mask=mask):
@@ -56,10 +56,10 @@
                 dst[hi] = out[half:]
                 return carry
 
-            lax.fori_loop(0, count // 2, pair, 0)
+            lax.fori_loop(0, count // 2, pair, 0, unroll=min(count // 2, unroll))
 
 
-def apply_levels(state, trp, pidx, masks, level_offset, layout, index_of, count, width, precision):
+def apply_levels(state, trp, pidx, masks, level_offset, layout, index_of, count, width, precision, unroll=1):
     rows = state.shape[-2]
     n_levels = len(masks)
     patterns = trp.shape[1]
@@ -67,7 +67,7 @@
     block = (count, None, rows, width) if state.ndim == 4 else (count, rows, width)
     flops = 2 * count * rows * 2 * rows * width * n_levels
     return pl.pallas_call(
-        functools.partial(levels_kernel, tuple(masks), level_offset, layout, precision),
+        functools.partial(levels_kernel, tuple(masks), level_offset, layout, precision, unroll),
         out_shape=jax.ShapeDtypeStruct((count, rows, width), state.dtype),
         grid_spec=pltpu.PrefetchScalarGridSpec(
             num_scalar_prefetch=1,
@@ -81,7 +81,8 @@
             out_specs=pl.BlockSpec(memory_space=pltpu.VMEM),
             scratch_shapes=[
                 pltpu.VMEM((patterns, 2, 2 * rank, 2 * rank), jnp.float32),
-                pltpu.VMEM((2, count, rows, width), jnp.float32),
+                pltpu.VMEM((count, rows, width), jnp.float32),
+                pltpu.VMEM((count, rows, width), jnp.float32),
             ],
         ),
         compiler_params=pltpu.CompilerParams(vmem_limit_bytes=48 * 1024 * 1024),
@@ -147,7 +148,8 @@
             if first_cross > 0:
                 state = apply_levels(
                     shaped, translations, pattern_index, local_masks, 0, local_layout, index_of, count, width,
-                    lax.Precision.HIGH if (parity, chunk) == (0, 0) else lax.Precision.HIGHEST,
+                    lax.Precision.HIGHEST,
+                    8 if (parity, chunk) == (0, 0) else 1,
                 )
             elif split > 1:
                 state = shaped[:, parity, :, chunk * width : (chunk + 1) * width]

time: 230 us -> 229 us (level)
  no operation moved by 1% of the time
where the time goes in v9:
time: 229 us
  waiting for transfers between devices  133 us (58%)
  Pallas kernels  63.2 us (28%)
  starting transfers between devices  21.6 us (9%)
  local copies, waits for them, and re-layouts  10.4 us (5%)
    all_to_all x2, waiting for transfers between devices, body(): lax.all_to_all(current, 'src', split_axis=0, concat_axis=0, tiled=True)  74.9 us
    pallas_call x4, Pallas kernels, apply_levels(): pl.pallas_call(functools.partial(levels_kernel, tuple(masks), level_offse...  60.2 us
    all_to_all x2, waiting for transfers between devices, body(): lax.all_to_all(state, 'src', split_axis=0, concat_axis=0, tiled=True)  58.4 us
    all_to_all x2, starting transfers between devices, body(): lax.all_to_all(state, 'src', split_axis=0, concat_axis=0, tiled=True)  11.6 us
    all_to_all x2, starting transfers between devices, body(): lax.all_to_all(current, 'src', split_axis=0, concat_axis=0, tiled=True)  10 us
    unnamed x16, local copies, waits for them, and re-layouts  8.89 us
  transfers between devices with their start and end apart: 4, of which 4 were waited for; matrix products, arithmetic and copies ran while one was open for 0% of the time, Pallas kernels for 22%

profile of v9, /device:TPU:15, one launch (start us, length us, event | category | flops | bytes accessed | tf_op | source)
XLA Modules:
  0.0 228.6 jit_solution(2514852837360761467)
XLA Ops:
  0.0 0.7 copy-done.6
  0.7 12.3 %shard_map.37 = f32[16,128,256]{2,1,0:T(8,128)S(1)} custom-call(s32[8,512]{1,0:T(8,128)S(1)} %copy-done.6, f32[8,8,2,2,64,64]{5,4,3,2,1,0:T(8,128)} %tr_ref.7, f32[16,2,128,256]{3,2,1,0:T(8,128)} %bitcast.6), custom_call_target="tpu_custom_call" | custom-call | flops 1073741824 | bytes 6291456 | tf_op jit(solution)/shard_map/pallas_call | solution.py:69
  13.0 0.0 copy-start.5
  13.0 1.3 copy-done.5
  14.4 6.7 %all-to-all-start = ((f32[16,128,256]{2,1,0:T(8,128)}), f32[16,128,256]{2,1,0:T(8,128)S(1)}, u32[]{:S(2)}, u32[]{:S(2)}) async-start(f32[16,128,256]{2,1,0:T(8,128)} %copy-done.5), calls=%async_computation | async-start | bytes 4194304 | tf_op jit(solution)/shard_map/all_to_all | solution.py:158
  21.0 0.0 copy-done.7
  21.0 16.5 %shard_map.40 = f32[16,128,256]{2,1,0:T(8,128)S(1)} custom-call(s32[8,512]{1,0:T(8,128)S(1)} %copy-done.7, f32[8,8,2,2,64,64]{5,4,3,2,1,0:T(8,128)} %tr_ref.7, f32[16,2,128,256]{3,2,1,0:T(8,128)} %bitcast.7), custom_call_target="tpu_custom_call" | custom-call | flops 1073741824 | bytes 6291456 | tf_op jit(solution)/shard_map/pallas_call | solution.py:69
  37.5 1.3 copy-done.4
  38.8 29.6 %all-to-all-done.x_ref = f32[16,128,256]{2,1,0:T(8,128)S(1)} async-done(((f32[16,128,256]{2,1,0:T(8,128)}), f32[16,128,256]{2,1,0:T(8,128)S(1)}, u32[]{:S(2)}, u32[]{:S(2)}) %all-to-all-start) | async-done | bytes 2097184 | tf_op jit(solution)/shard_map/all_to_all | solution.py:158
  68.5 1.3 copy-done
  69.8 4.9 %all-to-all-start.2 = ((f32[16,128,256]{2,1,0:T(8,128)}), f32[16,128,256]{2,1,0:T(8,128)S(1)}, u32[]{:S(2)}, u32[]{:S(2)}) async-start(f32[16,128,256]{2,1,0:T(8,128)} %copy-done.4), calls=%async_computation.2 | async-start | bytes 4194304 | tf_op jit(solution)/shard_map/all_to_all | solution.py:158
  74.7 1.6 copy-done.1
  76.3 15.7 %shard_map.38 = f32[16,128,256]{2,1,0:T(8,128)S(1)} custom-call(s32[8,512]{1,0:T(8,128)S(1)} %copy-done.7, f32[8,8,2,2,64,64]{5,4,3,2,1,0:T(8,128)} %tr_ref.7, f32[16,128,256]{2,1,0:T(8,128)S(1)} %copy-done.1), custom_call_target="tpu_custom_call" | custom-call | flops 1073741824 | bytes 6291456 | tf_op jit(solution)/shard_map/pallas_call | solution.py:69
  92.0 0.0 copy-start.2
  92.0 1.3 copy-done.2
  93.3 28.8 %all-to-all-done.2.x_ref = f32[16,128,256]{2,1,0:T(8,128)S(1)} async-done(((f32[16,128,256]{2,1,0:T(8,128)}), f32[16,128,256]{2,1,0:T(8,128)S(1)}, u32[]{:S(2)}, u32[]{:S(2)}) %all-to-all-start.2) | async-done | bytes 2097184 | tf_op jit(solution)/shard_map/all_to_all | solution.py:158
  122.1 5.1 %all-to-all-start.1 = ((f32[16,128,256]{2,1,0:T(8,128)}), f32[16,128,256]{2,1,0:T(8,128)}, u32[]{:S(2)}, u32[]{:S(2)}) async-start(f32[16,128,256]{2,1,0:T(8,128)} %copy-done.2), calls=%async_computation.1 | async-start | bytes 4194304 | tf_op jit(solution)/shard_map/all_to_all | solution.py:163
  127.2 15.7 %shard_map.41 = f32[16,128,256]{2,1,0:T(8,128)S(1)} custom-call(s32[8,512]{1,0:T(8,128)S(1)} %copy-done.7, f32[8,8,2,2,64,64]{5,4,3,2,1,0:T(8,128)} %tr_ref.7, f32[16,128,256]{2,1,0:T(8,128)S(1)} %all-to-all-done.2.x_ref), custom_call_target="tpu_custom_call" | custom-call | flops 1073741824 | bytes 6291456 | tf_op jit(solution)/shard_map/pallas_call | solution.py:69
  142.9 1.3 copy-done.3
  144.2 30.5 %all-to-all-done.1.x_ref = f32[16,128,256]{2,1,0:T(8,128)} async-done(((f32[16,128,256]{2,1,0:T(8,128)}), f32[16,128,256]{2,1,0:T(8,128)}, u32[]{:S(2)}, u32[]{:S(2)}) %all-to-all-start.1) | async-done | bytes 2097184 | tf_op jit(solution)/shard_map/all_to_all | solution.py:163
  174.7 4.9 %all-to-all-start.3 = ((f32[16,128,256]{2,1,0:T(8,128)}), f32[16,128,256]{2,1,0:T(8,128)S(1)}, u32[]{:S(2)}, u32[]{:S(2)}) async-start(f32[16,128,256]{2,1,0:T(8,128)} %copy-done.3), calls=%async_computation.3 | async-start | bytes 4194304 | tf_op jit(solution)/shard_map/all_to_all | solution.py:163
  179.6 3.0 %shard_map.39 = f32[16,2,128,256]{3,2,1,0:T(8,128)} custom-call(f32[16,128,256]{2,1,0:T(8,128)} %all-to-all-done.1.x_ref), custom_call_target="tpu_custom_call" | custom-call | bytes 4194304 | tf_op jit(solution)/shard_map/pallas_call | solution.py:110
  182.6 44.4 %all-to-all-done.3 = f32[16,128,256]{2,1,0:T(8,128)S(1)} async-done(((f32[16,128,256]{2,1,0:T(8,128)}), f32[16,128,256]{2,1,0:T(8,128)S(1)}, u32[]{:S(2)}, u32[]{:S(2)}) %all-to-all-start.3) | async-done | bytes 2097184 | tf_op jit(solution)/shard_map/all_to_all | solution.py:163
  227.0 1.5 bitcast_dynamic-update-slice_fusion
  (6 shorter events, 0.0 us)
Async XLA Ops:
  0.0 0.7 copy-start.6
  13.0 1.3 copy-start.5
  14.4 6.7 %copy-start.7 = (s32[8,512]{1,0:T(8,128)S(1)}, s32[8,512]{1,0:T(8,128)}, u32[]{:S(2)}) copy-start(s32[8,512]{1,0:T(8,128)} %pidx_ref.7) | copy-start | bytes 49156
  14.4 54.1 %all-to-all-start = ((f32[16,128,256]{2,1,0:T(8,128)}), f32[16,128,256]{2,1,0:T(8,128)S(1)}, u32[]{:S(2)}, u32[]{:S(2)}) async-start(f32[16,128,256]{2,1,0:T(8,128)} %copy-done.5), calls=%async_computation | async-start | bytes 4194304 | tf_op jit(solution)/shard_map/all_to_all | solution.py:158
  37.5 1.3 copy-start.4
  68.5 1.3 copy-start
  69.8 52.3 %all-to-all-start.2 = ((f32[16,128,256]{2,1,0:T(8,128)}), f32[16,128,256]{2,1,0:T(8,128)S(1)}, u32[]{:S(2)}, u32[]{:S(2)}) async-start(f32[16,128,256]{2,1,0:T(8,128)} %copy-done.4), calls=%async_computation.2 | async-start | bytes 4194304 | tf_op jit(solution)/shard_map/all_to_all | solution.py:158
  74.7 1.6 copy-start.1
  92.0 1.3 copy-start.2
  122.1 52.6 %all-to-all-start.1 = ((f32[16,128,256]{2,1,0:T(8,128)}), f32[16,128,256]{2,1,0:T(8,128)}, u32[]{:S(2)}, u32[]{:S(2)}) async-start(f32[16,128,256]{2,1,0:T(8,128)} %copy-done.2), calls=%async_computation.1 | async-start | bytes 4194304 | tf_op jit(solution)/shard_map/all_to_all | solution.py:163
  142.9 1.3 copy-start.3
  174.7 52.3 %all-to-all-start.3 = ((f32[16,128,256]{2,1,0:T(8,128)}), f32[16,128,256]{2,1,0:T(8,128)S(1)}, u32[]{:S(2)}, u32[]{:S(2)}) async-start(f32[16,128,256]{2,1,0:T(8,128)} %copy-done.3), calls=%async_computation.3 | async-start | bytes 4194304 | tf_op jit(solution)/shard_map/all_to_all | solution.py:163

commit v10 on v9

--- a/solution.py
+++ b/solution.py
@@ -148,7 +148,7 @@
             if first_cross > 0:
                 state = apply_levels(
                     shaped, translations, pattern_index, local_masks, 0, local_layout, index_of, count, width,
-                    lax.Precision.HIGHEST,
+                    lax.Precision.HIGH if (parity, chunk) == (0, 0) else lax.Precision.HIGHEST,
                     8 if (parity, chunk) == (0, 0) else 1,
                 )
             elif split > 1:

time: 229 us -> 225 us (0.983)
  Pallas kernels: 63.2 us -> 59.4 us
    pallas_call x4, Pallas kernels: 60.2 us -> 56.4 us  [apply_levels(): pl.pallas_call(functools.partial(levels_kernel, tuple(masks), level_offse...]
  transfers between devices with their start and end apart: 4 -> 4, of which waited for: 4 -> 4; matrix products, arithmetic and copies ran while one was open for 0% -> 0% of each run, Pallas kernels for 22% -> 23%
where the time goes in v10:
time: 225 us
  waiting for transfers between devices  133 us (59%)
  Pallas kernels  59.4 us (26%)
  starting transfers between devices  21.4 us (10%)
  local copies, waits for them, and re-layouts  10.4 us (5%)
    all_to_all x2, waiting for transfers between devices, body(): lax.all_to_all(current, 'src', split_axis=0, concat_axis=0, tiled=True)  74.9 us
    all_to_all x2, waiting for transfers between devices, body(): lax.all_to_all(state, 'src', split_axis=0, concat_axis=0, tiled=True)  58.4 us
    pallas_call x4, Pallas kernels, apply_levels(): pl.pallas_call(functools.partial(levels_kernel, tuple(masks), level_offse...  56.4 us
    all_to_all x2, starting transfers between devices, body(): lax.all_to_all(state, 'src', split_axis=0, concat_axis=0, tiled=True)  11.6 us
    all_to_all x2, starting transfers between devices, body(): lax.all_to_all(current, 'src', split_axis=0, concat_axis=0, tiled=True)  9.82 us
    unnamed x16, local copies, waits for them, and re-layouts  8.89 us
  transfers between devices with their start and end apart: 4, of which 4 were waited for; matrix products, arithmetic and copies ran while one was open for 0% of the time, Pallas kernels for 23%

profile of v10, /device:TPU:15, one launch (start us, length us, event | category | flops | bytes accessed | tf_op | source)
XLA Modules:
  0.0 224.6 jit_solution(8279224390637672857)
XLA Ops:
  0.0 0.7 copy-done.6
  0.7 8.5 %shard_map.37 = f32[16,128,256]{2,1,0:T(8,128)S(1)} custom-call(s32[8,512]{1,0:T(8,128)S(1)} %copy-done.6, f32[8,8,2,2,64,64]{5,4,3,2,1,0:T(8,128)} %tr_ref.7, f32[16,2,128,256]{3,2,1,0:T(8,128)} %bitcast.6), custom_call_target="tpu_custom_call" | custom-call | flops 1073741824 | bytes 6291456 | tf_op jit(solution)/shard_map/pallas_call | solution.py:69
  9.2 0.0 copy-start.5
  9.2 1.3 copy-done.5
  10.5 6.7 %all-to-all-start = ((f32[16,128,256]{2,1,0:T(8,128)}), f32[16,128,256]{2,1,0:T(8,128)S(1)}, u32[]{:S(2)}, u32[]{:S(2)}) async-start(f32[16,128,256]{2,1,0:T(8,128)} %copy-done.5), calls=%async_computation | async-start | bytes 4194304 | tf_op jit(solution)/shard_map/all_to_all | solution.py:158
  17.2 0.0 copy-done.7
  17.2 16.5 %shard_map.40 = f32[16,128,256]{2,1,0:T(8,128)S(1)} custom-call(s32[8,512]{1,0:T(8,128)S(1)} %copy-done.7, f32[8,8,2,2,64,64]{5,4,3,2,1,0:T(8,128)} %tr_ref.7, f32[16,2,128,256]{3,2,1,0:T(8,128)} %bitcast.7), custom_call_target="tpu_custom_call" | custom-call | flops 1073741824 | bytes 6291456 | tf_op jit(solution)/shard_map/pallas_call | solution.py:69
  33.7 1.3 copy-done.4
  35.0 29.6 %all-to-all-done.x_ref = f32[16,128,256]{2,1,0:T(8,128)S(1)} async-done(((f32[16,128,256]{2,1,0:T(8,128)}), f32[16,128,256]{2,1,0:T(8,128)S(1)}, u32[]{:S(2)}, u32[]{:S(2)}) %all-to-all-start) | async-done | bytes 2097184 | tf_op jit(solution)/shard_map/all_to_all | solution.py:158
  64.7 1.3 copy-done
  66.0 4.9 %all-to-all-start.2 = ((f32[16,128,256]{2,1,0:T(8,128)}), f32[16,128,256]{2,1,0:T(8,128)S(1)}, u32[]{:S(2)}, u32[]{:S(2)}) async-start(f32[16,128,256]{2,1,0:T(8,128)} %copy-done.4), calls=%async_computation.2 | async-start | bytes 4194304 | tf_op jit(solution)/shard_map/all_to_all | solution.py:158
  70.9 1.6 copy-done.1
  72.5 15.7 %shard_map.38 = f32[16,128,256]{2,1,0:T(8,128)S(1)} custom-call(s32[8,512]{1,0:T(8,128)S(1)} %copy-done.7, f32[8,8,2,2,64,64]{5,4,3,2,1,0:T(8,128)} %tr_ref.7, f32[16,128,256]{2,1,0:T(8,128)S(1)} %copy-done.1), custom_call_target="tpu_custom_call" | custom-call | flops 1073741824 | bytes 6291456 | tf_op jit(solution)/shard_map/pallas_call | solution.py:69
  88.2 0.0 copy-start.2
  88.2 1.3 copy-done.2
  89.5 28.8 %all-to-all-done.2.x_ref = f32[16,128,256]{2,1,0:T(8,128)S(1)} async-done(((f32[16,128,256]{2,1,0:T(8,128)}), f32[16,128,256]{2,1,0:T(8,128)S(1)}, u32[]{:S(2)}, u32[]{:S(2)}) %all-to-all-start.2) | async-done | bytes 2097184 | tf_op jit(solution)/shard_map/all_to_all | solution.py:158
  118.3 4.9 %all-to-all-start.1 = ((f32[16,128,256]{2,1,0:T(8,128)}), f32[16,128,256]{2,1,0:T(8,128)}, u32[]{:S(2)}, u32[]{:S(2)}) async-start(f32[16,128,256]{2,1,0:T(8,128)} %copy-done.2), calls=%async_computation.1 | async-start | bytes 4194304 | tf_op jit(solution)/shard_map/all_to_all | solution.py:163
  123.2 15.7 %shard_map.41 = f32[16,128,256]{2,1,0:T(8,128)S(1)} custom-call(s32[8,512]{1,0:T(8,128)S(1)} %copy-done.7, f32[8,8,2,2,64,64]{5,4,3,2,1,0:T(8,128)} %tr_ref.7, f32[16,128,256]{2,1,0:T(8,128)S(1)} %all-to-all-done.2.x_ref), custom_call_target="tpu_custom_call" | custom-call | flops 1073741824 | bytes 6291456 | tf_op jit(solution)/shard_map/pallas_call | solution.py:69
  138.9 1.3 copy-done.3
  140.2 30.5 %all-to-all-done.1.x_ref = f32[16,128,256]{2,1,0:T(8,128)} async-done(((f32[16,128,256]{2,1,0:T(8,128)}), f32[16,128,256]{2,1,0:T(8,128)}, u32[]{:S(2)}, u32[]{:S(2)}) %all-to-all-start.1) | async-done | bytes 2097184 | tf_op jit(solution)/shard_map/all_to_all | solution.py:163
  170.7 4.9 %all-to-all-start.3 = ((f32[16,128,256]{2,1,0:T(8,128)}), f32[16,128,256]{2,1,0:T(8,128)S(1)}, u32[]{:S(2)}, u32[]{:S(2)}) async-start(f32[16,128,256]{2,1,0:T(8,128)} %copy-done.3), calls=%async_computation.3 | async-start | bytes 4194304 | tf_op jit(solution)/shard_map/all_to_all | solution.py:163
  175.6 3.0 %shard_map.39 = f32[16,2,128,256]{3,2,1,0:T(8,128)} custom-call(f32[16,128,256]{2,1,0:T(8,128)} %all-to-all-done.1.x_ref), custom_call_target="tpu_custom_call" | custom-call | bytes 4194304 | tf_op jit(solution)/shard_map/pallas_call | solution.py:110
  178.6 44.4 %all-to-all-done.3 = f32[16,128,256]{2,1,0:T(8,128)S(1)} async-done(((f32[16,128,256]{2,1,0:T(8,128)}), f32[16,128,256]{2,1,0:T(8,128)S(1)}, u32[]{:S(2)}, u32[]{:S(2)}) %all-to-all-start.3) | async-done | bytes 2097184 | tf_op jit(solution)/shard_map/all_to_all | solution.py:163
  223.1 1.5 bitcast_dynamic-update-slice_fusion
  (6 shorter events, 0.0 us)
Async XLA Ops:
  0.0 0.7 copy-start.6
  9.2 1.3 copy-start.5
  10.5 6.7 %copy-start.7 = (s32[8,512]{1,0:T(8,128)S(1)}, s32[8,512]{1,0:T(8,128)}, u32[]{:S(2)}) copy-start(s32[8,512]{1,0:T(8,128)} %pidx_ref.7) | copy-start | bytes 49156
  10.5 54.1 %all-to-all-start = ((f32[16,128,256]{2,1,0:T(8,128)}), f32[16,128,256]{2,1,0:T(8,128)S(1)}, u32[]{:S(2)}, u32[]{:S(2)}) async-start(f32[16,128,256]{2,1,0:T(8,128)} %copy-done.5), calls=%async_computation | async-start | bytes 4194304 | tf_op jit(solution)/shard_map/all_to_all | solution.py:158
  33.7 1.3 copy-start.4
  64.7 1.3 copy-start
  66.0 52.3 %all-to-all-start.2 = ((f32[16,128,256]{2,1,0:T(8,128)}), f32[16,128,256]{2,1,0:T(8,128)S(1)}, u32[]{:S(2)}, u32[]{:S(2)}) async-start(f32[16,128,256]{2,1,0:T(8,128)} %copy-done.4), calls=%async_computation.2 | async-start | bytes 4194304 | tf_op jit(solution)/shard_map/all_to_all | solution.py:158
  70.9 1.6 copy-start.1
  88.2 1.3 copy-start.2
  118.3 52.4 %all-to-all-start.1 = ((f32[16,128,256]{2,1,0:T(8,128)}), f32[16,128,256]{2,1,0:T(8,128)}, u32[]{:S(2)}, u32[]{:S(2)}) async-start(f32[16,128,256]{2,1,0:T(8,128)} %copy-done.2), calls=%async_computation.1 | async-start | bytes 4194304 | tf_op jit(solution)/shard_map/all_to_all | solution.py:163
  138.9 1.3 copy-start.3
  170.7 52.3 %all-to-all-start.3 = ((f32[16,128,256]{2,1,0:T(8,128)}), f32[16,128,256]{2,1,0:T(8,128)S(1)}, u32[]{:S(2)}, u32[]{:S(2)}) async-start(f32[16,128,256]{2,1,0:T(8,128)} %copy-done.3), calls=%async_computation.3 | async-start | bytes 4194304 | tf_op jit(solution)/shard_map/all_to_all | solution.py:163
